TPU v7x, 128 devices: a whole 4x4x4 slice. The times are simulated.
128 devices in a mesh: req: 16 (over z, x), exp: 8 (over y, core).
Axes of the slice: x: 4, y: 4, z: 4, core: 2. Of those that a mesh axis runs over, the one named last changes fastest.
Arguments:
- tokens: bfloat16 [12288, 2880], P(('req', 'exp')), may hold values from -6 to 6
- attn_gain: float32 [2880], replicated, may hold values from 0.5 to 8
- w_query: bfloat16 [2880, 4096], P(None, 'exp'), may hold values from -0.109375 to 0.109375
- key_weight: bfloat16 [2880, 512], P(None, 'exp'), may hold values from -0.109375 to 0.109375
- value_weight: bfloat16 [2880, 512], P(None, 'exp'), may hold values from -0.109375 to 0.109375
- sinks: float32 [64], P('exp'), may hold values from -1 to 3
- w_out: bfloat16 [4096, 2880], P('exp'), may hold values from -0.09375 to 0.09375
- ffn_gain: float32 [2880], replicated, may hold values from 0.25 to 1.75
- router: bfloat16 [2880, 32], replicated, may hold values from -0.109375 to 0.109375
- routes: int32 [12288, 4], P(('req', 'exp')), may hold values from 0 to 31, all different within a row; in each aligned block of 96 rows (0 to 95, 96 to 191, ...) at most 14 rows name the same one
- lengths: int32 [16, 6], P('req'), may hold values from 1 to 384, 768 in all within a row
- expert_gate: bfloat16 [128, 2880, 720], P(('req', 'exp')), may hold values from -0.109375 to 0.109375
- expert_up: bfloat16 [128, 2880, 720], P(('req', 'exp')), may hold values from -0.109375 to 0.109375
- expert_down: bfloat16 [128, 720, 2880], P(('req', 'exp')), may hold values from -0.109375 to 0.109375
Outputs:
- layer_out: bfloat16 [12288, 2880], P(('req', 'exp'))
Inputs may be any that keep to these rules, and one draw needn't show every extreme that they name: `routes`: in the rows of one device no expert is named by more than 14 rows, a bound that some block reaches; a row names 4 different experts.
All inputs are finite; a program needn't handle non-finite values.
Results may differ from a plain program's by a relative error of at most 0.02.
The roundings to bfloat16 on the way count: a program that leaves them out, or rounds other values in their place, can miss the bound.
Values may be sent and summed in bfloat16 or wider, within the bound.
No kernel may reach another device: no remote copies, remote signals or barrier semaphores. Data moves between devices by JAX's collectives and lax.ppermute only.
A program may use at most 192 MiB of HBM per device.

v0:
```python
import jax
import jax.numpy as jnp
from jax import lax
from jax.sharding import PartitionSpec as P

QUERY_HEADS = 64
KEY_VALUE_HEADS = 8
HEAD_DIM = 64
EXPERTS = 32
TOPK = 4
CAP = 14


def rms_norm(value_rows, gain):
    mean_sq = jnp.mean(value_rows * value_rows, axis=-1, keepdims=True)
    return value_rows * lax.rsqrt(mean_sq + 1e-05) * gain


def rotate(value_rows, offset):
    half = value_rows.shape[-1] // 2
    freqs = jnp.exp(
        -(2.0 * jnp.arange(half, dtype=jnp.float32) / value_rows.shape[-1])
        * jnp.log(jnp.float32(150000.0))
    )
    angle = offset.astype(jnp.float32)[:, None] * freqs[None, :]
    cosine = jnp.cos(angle)[:, None, :]
    sine = jnp.sin(angle)[:, None, :]
    first = value_rows[..., :half]
    second = value_rows[..., half:]
    return jnp.concatenate(
        [first * cosine - second * sine, second * cosine + first * sine], axis=-1
    )


def per_device(
    tokens,
    attn_gain,
    w_query,
    key_weight,
    value_weight,
    sinks,
    w_out,
    ffn_gain,
    router,
    routes,
    lengths,
    expert_gate,
    expert_up,
    expert_down,
):
    tok_rows = tokens.shape[0]
    model_width = tokens.shape[1]
    local_heads = w_query.shape[1] // HEAD_DIM
    local_kv = key_weight.shape[1] // HEAD_DIM
    head_group = QUERY_HEADS // KEY_VALUE_HEADS
    normed_input = rms_norm(tokens.astype(jnp.float32), attn_gain).astype(jnp.bfloat16)
    piece = lax.all_gather(normed_input, "exp", axis=0, tiled=True)
    projected = jnp.concatenate(
        [
            jnp.dot(piece, w_query, preferred_element_type=jnp.float32),
            jnp.dot(piece, key_weight, preferred_element_type=jnp.float32),
            jnp.dot(piece, value_weight, preferred_element_type=jnp.float32),
        ],
        axis=1,
    )
    item_count = projected.shape[0]
    lens = lengths[0]
    ends = jnp.cumsum(lens)
    starts = ends - lens
    position = jnp.arange(item_count, dtype=jnp.int32)
    member = ((position[:, None] >= starts[None, :]) & (position[:, None] < ends[None, :])).astype(
        jnp.int32
    )
    segment = jnp.sum(member * jnp.arange(lens.shape[0], dtype=jnp.int32)[None, :], axis=1)
    offset = position - jnp.sum(member * starts[None, :], axis=1)
    q_width = local_heads * HEAD_DIM
    kv_width = local_kv * HEAD_DIM
    query_rows = rotate(
        projected[:, :q_width].reshape(item_count, local_heads, HEAD_DIM), offset
    ).astype(jnp.bfloat16)
    key_rows = rotate(
        projected[:, q_width : q_width + kv_width].reshape(item_count, local_kv, HEAD_DIM), offset
    ).astype(jnp.bfloat16)
    value_rows = (
        projected[:, q_width + kv_width :]
        .reshape(item_count, local_kv, HEAD_DIM)
        .astype(jnp.bfloat16)
    )
    grouped_heads = query_rows.reshape(item_count, local_kv, head_group, HEAD_DIM)
    scores = jnp.einsum(
        "qcgd,kcd->cgqk", grouped_heads, key_rows, preferred_element_type=jnp.float32
    ) * HEAD_DIM ** (-0.5)
    allowed = (segment[:, None] == segment[None, :]) & (position[None, :] <= position[:, None])
    sink_score_logit = sinks.reshape(local_kv, head_group, 1, 1)
    masked = jnp.where(allowed[None, None], scores, -jnp.inf)
    top = jnp.maximum(jnp.max(masked, axis=-1, keepdims=True), sink_score_logit)
    expo = jnp.where(allowed[None, None], jnp.exp(scores - top), 0.0)
    denom = jnp.sum(expo, axis=-1, keepdims=True) + jnp.exp(sink_score_logit - top)
    probs = (expo / denom).astype(jnp.bfloat16)
    attended = jnp.einsum("cgqk,kcd->qcgd", probs, value_rows, preferred_element_type=jnp.float32)
    attended = attended.reshape(item_count, q_width).astype(jnp.bfloat16)
    attn_sum = lax.psum_scatter(
        jnp.dot(attended, w_out, preferred_element_type=jnp.float32).astype(jnp.bfloat16),
        "exp",
        scatter_dimension=0,
        tiled=True,
    ).astype(jnp.float32)
    residual = (tokens.astype(jnp.float32) + attn_sum).astype(jnp.bfloat16)
    normed2 = rms_norm(residual.astype(jnp.float32), ffn_gain).astype(jnp.bfloat16)
    logits = jnp.dot(normed2, router, preferred_element_type=jnp.float32)
    picked = jnp.take_along_axis(logits, routes, axis=1)
    weights = jax.nn.softmax(picked, axis=-1)
    flat_routes = routes.reshape(-1)
    expert_ids = jnp.arange(EXPERTS, dtype=jnp.int32)
    onehot_route = (flat_routes[:, None] == expert_ids[None, :]).astype(jnp.int32)
    rank = jnp.cumsum(onehot_route, axis=0) - 1
    slot_rank = jnp.sum(onehot_route * rank, axis=1)
    flat_slot = flat_routes * CAP + slot_rank
    slot_ids = jnp.arange(EXPERTS * CAP, dtype=jnp.int32)
    dispatch_table = (slot_ids[:, None] == flat_slot[None, :]).astype(jnp.bfloat16)
    repeated = jnp.repeat(normed2, TOPK, axis=0)
    packed = jnp.dot(dispatch_table, repeated, preferred_element_type=jnp.float32).astype(
        jnp.bfloat16
    )
    n_req = lax.axis_size("req")
    n_exp = lax.axis_size("exp")
    devices = n_req * n_exp
    split = devices // EXPERTS
    send_rows = jnp.broadcast_to(
        packed.reshape(EXPERTS, 1, CAP, model_width), (EXPERTS, split, CAP, model_width)
    ).reshape(devices, CAP, model_width)
    received = lax.all_to_all(send_rows, ("req", "exp"), split_axis=0, concat_axis=0, tiled=True)
    flat_rows = received.reshape(-1, model_width)
    gate = jnp.dot(flat_rows, expert_gate[0], preferred_element_type=jnp.float32)
    up_val = jnp.dot(flat_rows, expert_up[0], preferred_element_type=jnp.float32)
    hidden = ((up_val + 1.0) * gate * jax.nn.sigmoid(1.702 * gate)).astype(jnp.bfloat16)
    slice_out = jnp.dot(hidden, expert_down[0], preferred_element_type=jnp.float32).astype(
        jnp.bfloat16
    )
    returned = lax.all_to_all(
        slice_out.reshape(received.shape), ("req", "exp"), split_axis=0, concat_axis=0, tiled=True
    )
    summed = returned.astype(jnp.float32).reshape(EXPERTS, split, CAP, model_width).sum(axis=1)
    summed = summed.reshape(EXPERTS * CAP, model_width)
    picked_rows = jnp.take(summed, flat_slot, axis=0).reshape(tok_rows, TOPK, model_width)
    moe_sum = jnp.sum(weights[:, :, None] * picked_rows, axis=1)
    return (residual.astype(jnp.float32) + moe_sum).astype(jnp.bfloat16)


def solution(mesh):
    return jax.shard_map(
        per_device,
        mesh=mesh,
        in_specs=(
            P(("req", "exp"), None),
            P(),
            P(None, "exp"),
            P(None, "exp"),
            P(None, "exp"),
            P("exp"),
            P("exp", None),
            P(),
            P(),
            P(("req", "exp"), None),
            P("req", None),
            P(("req", "exp"), None, None),
            P(("req", "exp"), None, None),
            P(("req", "exp"), None, None),
        ),
        out_specs=P(("req", "exp"), None),
        check_vma=False,
    )
```

profile of v0, /device:TPU:10, one launch (start us, length us, event | category | flops | bytes accessed | tf_op | source)
XLA Modules:
  0.0 587.1 jit_solution(4064006883043466249)
XLA Ops:
  6.5 1.4 fusion.19
  8.0 2.1 fusion.21
  11.7 1.1 multiply_cosine_fusion
  13.2 31.8 %all-gather.2.cloned.1.call-done = bf16[768,2880]{1,0:T(8,128)(2,1)} async-done(((bf16[96,2880]{1,0:T(8,128)(2,1)}), bf16[768,2880]{1,0:T(8,128)(2,1)}) %all-gather.2.cloned.1.call-update) | async-done | bytes 4423696 | tf_op jit(solution)/shard_map/all_gather | solution.py:57
  45.0 3.9 convolution_bitcast_fusion
  49.4 4.6 fusion.59
  54.3 8.7 %fusion = (f32[8,768]{1,0:T(8,128)S(1)}, f32[768,768,8]{1,0,2:T(8,128)}) fusion(pred[768,768]{0,1:T(8,128)(4,1)S(1)} %fusion.13, bf16[768,8,32]{0,2,1:T(8,128)(2,1)S(1)} %get-tuple-element.10, bf16[768,8,32]{0,2,1:T(8,128)(2,1)S(1)} %get-tuple-element.9, bf16[768,32]{0,1:T(8,128)(2,1)S(1)} %get-tuple-element.12, bf16[768,32]{0,1:T(8,128)(2,1)S(1)} %get-tuple-element.11), kind=kOutput, calls=%fused_computation.5 | convolution fusion | flops 619898880 | bytes 20373504 | tf_op jit(solution)/shard_map/qcgd,kcd->cgqk/dot_general | solution.py:90
  64.2 10.8 %fusion.3 = f32[8,768]{1,0:T(8,128)} fusion(f32[768,768,8]{1,0,2:T(8,128)} %get-tuple-element.16, f32[8,768]{1,0:T(8,128)} %broadcast_maximum_fusion, pred[768,768]{0,1:T(8,128)(4,1)S(1)} %fusion.13), kind=kLoop, calls=%fused_computation.9 | loop fusion | flops 18868224 | bytes 19513344 | tf_op jit(solution)/shard_map/reduce_sum | solution.py:98
  75.0 1.4 exponential_add_fusion
  76.5 14.1 %fusion.16 = bf16[64,8,768]{2,0,1:T(8,128)(2,1)} fusion(f32[8,768]{1,0:T(8,128)} %exponential_add_fusion, f32[8,768]{1,0:T(8,128)} %broadcast_maximum_fusion, f32[768,768,8]{1,0,2:T(8,128)} %get-tuple-element.16, pred[768,768]{0,1:T(8,128)(4,1)S(1)} %fusion.13, bf16[768,2880]{1,0:T(8,128)(2,1)} %all-gather.2.cloned.1.call-done, bf16[2880,64]{0,1:T(8,128)(2,1)} %param.18), kind=kOutput, calls=%fused_computation.30 | convolution fusion | flops 911130624 | bytes 25092096 | tf_op jit(solution)/shard_map/cgqk,kcd->qcgd/dot_general | solution.py:100
  90.5 5.8 convolution_convert_fusion.1
  98.8 33.6 %reduce-scatter.2.cloned.1.call-done = bf16[96,2880]{1,0:T(8,128)(2,1)} async-done(((bf16[768,2880]{1,0:T(8,128)(2,1)}), bf16[96,2880]{1,0:T(8,128)(2,1)}) %reduce-scatter.2.cloned.1.call-update) | async-done | bytes 552976 | tf_op jit(solution)/shard_map/reduce_scatter | solution.py:102
  132.4 1.3 fusion.23
  133.8 1.3 fusion.25
  135.7 2.4 reshape.417
  138.1 4.7 convolution_convert_fusion.2
  142.8 4.4 broadcast_in_dim.41
  147.3 7.1 %broadcast_in_dim.42 = bf16[32,4,14,2880]{3,2,1,0:T(8,128)(2,1)} broadcast(bf16[32,14,2880]{2,1,0:T(8,128)(2,1)} %broadcast_in_dim.41), dimensions={0,2,3} | broadcast | bytes 12902400 | tf_op jit(solution)/shard_map/broadcast_in_dim | solution.py:129
  154.4 145.1 %all_to_all.10 = bf16[128,14,2880]{2,1,0:T(8,128)(2,1)} all-to-all(bf16[128,14,2880]{2,1,0:T(8,128)(2,1)} %bitcast.104), channel_id=1, replica_groups=mesh['req'=16,'exp'=8] {'req','exp'}, dimensions={0} | all-to-all | bytes 20643840 | tf_op jit(solution)/shard_map/all_to_all | solution.py:132
  299.5 15.4 %reshape.419 = bf16[1792,2880]{1,0:T(8,128)(2,1)} reshape(bf16[128,14,2880]{2,1,0:T(8,128)(2,1)} %all_to_all.10) | data formatting | bytes 20643840 | tf_op jit(solution)/shard_map/reshape | solution.py:133
  314.8 14.6 %fusion.7 = f32[1792,720]{0,1:T(8,128)} fusion(bf16[1792,2880]{1,0:T(8,128)(2,1)} %reshape.419, bf16[1,2880,720]{1,2,0:T(8,128)(2,1)} %param.25), kind=kOutput, calls=%fused_computation.18 | convolution fusion | flops 7431782400 | bytes 19630080 | tf_op jit(solution)/shard_map/dot_general | solution.py:134
  329.4 27.2 %convolution_convert_fusion = bf16[1792,2880]{0,1:T(8,128)(2,1)} fusion(bf16[1,720,2880]{2,1,0:T(8,128)(2,1)} %param.27, f32[1792,720]{0,1:T(8,128)} %fusion.7, bf16[1792,2880]{1,0:T(8,128)(2,1)} %reshape.419, bf16[1,2880,720]{1,2,0:T(8,128)(2,1)} %param.26), kind=kOutput, calls=%fused_computation.10 | convolution fusion | flops 14879047680 | bytes 34099200 | tf_op jit(solution)/shard_map/dot_general | solution.py:137
  356.7 14.3 %copy.49 = bf16[1792,2880]{1,0:T(8,128)(2,1)} copy(bf16[1792,2880]{0,1:T(8,128)(2,1)} %convolution_convert_fusion) | data formatting | bytes 20643840 | tf_op jit(solution)/shard_map/convert_element_type | solution.py:137
  371.0 14.4 %reshape.420 = bf16[128,14,2880]{2,1,0:T(8,128)(2,1)} reshape(bf16[1792,2880]{1,0:T(8,128)(2,1)} %copy.49) | data formatting | bytes 20643840 | tf_op jit(solution)/shard_map/reshape | solution.py:141
  385.4 9.1 %all-to-all-start.1 = ((bf16[128,14,2880]{2,1,0:T(8,128)(2,1)}), bf16[128,14,2880]{2,1,0:T(8,128)(2,1)}, u32[]{:S(2)}, u32[]{:S(2)}) async-start(bf16[128,14,2880]{2,1,0:T(8,128)(2,1)} %reshape.420), calls=%async_computation.2 | async-start | bytes 24117248 | tf_op jit(solution)/shard_map/all_to_all | solution.py:140
  395.7 2.9 gather_fusion.1
  399.6 142.9 %all-to-all-done.1 = bf16[128,14,2880]{2,1,0:T(8,128)(2,1)} async-done(((bf16[128,14,2880]{2,1,0:T(8,128)(2,1)}), bf16[128,14,2880]{2,1,0:T(8,128)(2,1)}, u32[]{:S(2)}, u32[]{:S(2)}) %all-to-all-start.1) | async-done | bytes 10321952 | tf_op jit(solution)/shard_map/all_to_all | solution.py:140
  542.5 9.8 %convert_reduce_fusion = f32[32,14,2880]{2,1,0:T(8,128)} fusion(bf16[128,14,2880]{2,1,0:T(8,128)(2,1)} %all-to-all-done.1), kind=kLoop, calls=%fused_computation.2 | loop fusion | flops 9031680 | bytes 15482880 | tf_op jit(solution)/shard_map/reduce_sum | solution.py:143
  552.3 5.6 reshape.423
  557.9 9.1 %gather_fusion = f32[384,2880]{1,0:T(8,128)} fusion(f32[448,2880]{1,0:T(8,128)} %reshape.423, s32[1024]{0:T(1024)S(1)} %pad_clamp_fusion), kind=kCustom, calls=%fused_computation | custom fusion | bytes 8848896 | tf_op jit(solution)/shard_map/jit(_take)/gather | solution.py:145
  567.0 5.5 gather.12
  572.5 6.5 %multiply_reduce_fusion = f32[96,2880]{1,0:T(8,128)S(1)} fusion(f32[96,4,2880]{2,1,0:T(4,128)} %gather.12, f32[96,4]{1,0:T(8,128)} %copy.43, pred[96,4]{1,0:T(8,128)(4,1)S(1)} %copy.48), kind=kLoop, calls=%fused_computation.15 | loop fusion | flops 3041280 | bytes 5531520 | tf_op jit(solution)/shard_map/reduce_sum | solution.py:146
  (69 shorter events, 10.0 us)
Async XLA Ops:
  6.5 84.0 %copy-start = (bf16[512,2880]{0,1:T(8,128)(2,1)S(1)}, bf16[512,2880]{0,1:T(8,128)(2,1)}, u32[]{:S(2)}) copy-start(bf16[512,2880]{0,1:T(8,128)(2,1)} %param.20) | copy-start | bytes 8847364
  6.5 38.5 %all-gather.2.cloned.1.call-start = ((), (), s32[]{:S(2)}) async-start(), calls=%async_computation.3 | async-start | bytes 5087232 | tf_op jit(solution)/shard_map/all_gather | solution.py:57
  10.1 122.3 %reduce-scatter.2.cloned.1.call-start = ((), (), s32[]{:S(2)}) async-start(), calls=%async_computation.4 | async-start | bytes 5087232 | tf_op jit(solution)/shard_map/reduce_scatter | solution.py:102
  45.0 4.4 copy-start.4
  49.4 4.7 copy-start.5
  49.4 4.7 copy-start.6
  54.3 9.3 %copy-start.11 = (f32[8]{0:T(128)S(1)}, f32[8]{0:T(128)}, u32[]{:S(2)}) copy-start(f32[8]{0:T(128)} %param.19) | copy-start | bytes 100
  62.9 0.6 copy-start.7
  96.4 0.7 copy-start.9
  96.4 36.1 %copy-start.2 = (bf16[96,2880]{1,0:T(8,128)(2,1)S(1)}, bf16[96,2880]{1,0:T(8,128)(2,1)}, u32[]{:S(2)}) copy-start(bf16[96,2880]{1,0:T(8,128)(2,1)} %param.14) | copy-start | bytes 1658884
  96.4 37.4 %copy-start.10 = (f32[2880]{0:T(1024)S(1)}, f32[2880]{0:T(1024)}, u32[]{:S(2)}) copy-start(f32[2880]{0:T(1024)} %param.21) | copy-start | bytes 34564
  385.4 10.0 %copy-start.8 = (bf16[2880,32]{0,1:T(8,128)(2,1)S(1)}, bf16[2880,32]{0,1:T(8,128)(2,1)}, u32[]{:S(2)}) copy-start(bf16[2880,32]{0,1:T(8,128)(2,1)} %param.22) | copy-start | bytes 552964
  385.4 157.1 %all-to-all-start.1 = ((bf16[128,14,2880]{2,1,0:T(8,128)(2,1)}), bf16[128,14,2880]{2,1,0:T(8,128)(2,1)}, u32[]{:S(2)}, u32[]{:S(2)}) async-start(bf16[128,14,2880]{2,1,0:T(8,128)(2,1)} %reshape.420), calls=%async_computation.2 | async-start | bytes 24117248 | tf_op jit(solution)/shard_map/all_to_all | solution.py:140
  567.0 13.1 %copy-start.1 = (bf16[512,2880]{0,1:T(8,128)(2,1)S(1)}, bf16[512,2880]{0,1:T(8,128)(2,1)}, u32[]{:S(2)}) copy-start(bf16[512,2880]{0,1:T(8,128)(2,1)} %param.20) | copy-start | bytes 8847364
  572.5 6.5 %copy-start.3 = (bf16[96,2880]{1,0:T(8,128)(2,1)S(1)}, bf16[96,2880]{1,0:T(8,128)(2,1)}, u32[]{:S(2)}) copy-start(bf16[96,2880]{1,0:T(8,128)(2,1)} %reduce-scatter.2.cloned.1.call-done) | copy-start | bytes 1658884
Sparse Core Ops, SparseCore 0:
  10.2 34.7 all-gather.1
  96.5 35.8 reduce-scatter.1
where the time goes:
time: 594 us; the launch traced here: 587 us
  waiting for transfers between devices  208 us (35%)
  blocking collectives  145 us (24%)
  local copies, waits for them, and re-layouts  85.3 us (14%)
  matrix products  83.9 us (14%)
  other arithmetic  41.3 us (7%)
  between operations  13.9 us (2%)
  starting transfers between devices  9.16 us (2%)
    all_to_all x1, blocking collectives, per_device(): lax.all_to_all(send_rows, ('req', 'exp'), split_axis=0, concat_axis=0, ti...  145 us
    all_to_all x1, waiting for transfers between devices, per_device(): lax.all_to_all(slice_out.reshape(received.shape), ('req', 'exp'), split_a...  143 us
    reduce_scatter x1, waiting for transfers between devices, per_device(): lax.psum_scatter(jnp.dot(attended, w_out, preferred_element_type=jnp.floa...  33.6 us
    all_gather x1, waiting for transfers between devices, per_device(): piece = lax.all_gather(normed_input, 'exp', axis=0, tiled=True)  31.8 us
    dot_general x1, matrix products, per_device(): jnp.dot(hidden, expert_down[0], preferred_element_type=jnp.float32)  27.2 us
    reshape x1, local copies, waits for them, and re-layouts, per_device(): flat_rows = received.reshape(-1, model_width)  15.4 us
    gather x2, local copies, waits for them, and re-layouts, per_device(): jnp.take(summed, flat_slot, axis=0).reshape(tok_rows, TOPK, model_width)  14.6 us
    dot_general x1, matrix products, per_device(): jnp.dot(flat_rows, expert_gate[0], preferred_element_type=jnp.float32)  14.6 us
  transfers between devices with their start and end apart: 3, of which 3 were waited for; matrix products, arithmetic and copies ran while one was open for 2% of the time, Pallas kernels for 0%

commit v1 on v0

--- a/solution.py
+++ b/solution.py
@@ -54,7 +54,8 @@
     local_kv = key_weight.shape[1] // HEAD_DIM
     head_group = QUERY_HEADS // KEY_VALUE_HEADS
     normed_input = rms_norm(tokens.astype(jnp.float32), attn_gain).astype(jnp.bfloat16)
-    piece = lax.all_gather(normed_input, "exp", axis=0, tiled=True)
+    by_chip = lax.all_gather(normed_input, "y", axis=0, tiled=False)
+    piece = lax.all_gather(by_chip, "c", axis=1, tiled=True).reshape(-1, model_width)
     projected = jnp.concatenate(
         [
             jnp.dot(piece, w_query, preferred_element_type=jnp.float32),
@@ -99,12 +100,14 @@
     probs = (expo / denom).astype(jnp.bfloat16)
     attended = jnp.einsum("cgqk,kcd->qcgd", probs, value_rows, preferred_element_type=jnp.float32)
     attended = attended.reshape(item_count, q_width).astype(jnp.bfloat16)
+    head_term = jnp.dot(attended, w_out, preferred_element_type=jnp.float32).astype(jnp.bfloat16)
+    n_y = lax.axis_size("y")
+    n_c = lax.axis_size("c")
+    head_term = head_term.reshape(n_y, n_c, tok_rows, model_width).transpose(1, 0, 2, 3)
+    on_chip = lax.psum_scatter(head_term, "c", scatter_dimension=0, tiled=True)
     attn_sum = lax.psum_scatter(
-        jnp.dot(attended, w_out, preferred_element_type=jnp.float32).astype(jnp.bfloat16),
-        "exp",
-        scatter_dimension=0,
-        tiled=True,
-    ).astype(jnp.float32)
+        on_chip.reshape(n_y, tok_rows, model_width), "y", scatter_dimension=0, tiled=True
+    ).reshape(tok_rows, model_width).astype(jnp.float32)
     residual = (tokens.astype(jnp.float32) + attn_sum).astype(jnp.bfloat16)
     normed2 = rms_norm(residual.astype(jnp.float32), ffn_gain).astype(jnp.bfloat16)
     logits = jnp.dot(normed2, router, preferred_element_type=jnp.float32)
@@ -122,25 +125,25 @@
     packed = jnp.dot(dispatch_table, repeated, preferred_element_type=jnp.float32).astype(
         jnp.bfloat16
     )
-    n_req = lax.axis_size("req")
-    n_exp = lax.axis_size("exp")
-    devices = n_req * n_exp
-    split = devices // EXPERTS
+    halves = n_y // (EXPERTS // lax.axis_size("req"))
     send_rows = jnp.broadcast_to(
-        packed.reshape(EXPERTS, 1, CAP, model_width), (EXPERTS, split, CAP, model_width)
-    ).reshape(devices, CAP, model_width)
-    received = lax.all_to_all(send_rows, ("req", "exp"), split_axis=0, concat_axis=0, tiled=True)
-    flat_rows = received.reshape(-1, model_width)
+        packed.reshape(EXPERTS, 1, CAP, model_width), (EXPERTS, halves, CAP, model_width)
+    ).reshape(EXPERTS * halves, CAP, model_width)
+    received = lax.all_to_all(send_rows, ("req", "y"), split_axis=0, concat_axis=0, tiled=True)
+    both = lax.all_gather(received, "c", axis=0, tiled=False)
+    flat_rows = both.reshape(-1, model_width)
     gate = jnp.dot(flat_rows, expert_gate[0], preferred_element_type=jnp.float32)
     up_val = jnp.dot(flat_rows, expert_up[0], preferred_element_type=jnp.float32)
     hidden = ((up_val + 1.0) * gate * jax.nn.sigmoid(1.702 * gate)).astype(jnp.bfloat16)
     slice_out = jnp.dot(hidden, expert_down[0], preferred_element_type=jnp.float32).astype(
         jnp.bfloat16
     )
-    returned = lax.all_to_all(
-        slice_out.reshape(received.shape), ("req", "exp"), split_axis=0, concat_axis=0, tiled=True
+    swapped = lax.all_to_all(
+        slice_out.reshape(both.shape), "c", split_axis=0, concat_axis=0, tiled=True
     )
-    summed = returned.astype(jnp.float32).reshape(EXPERTS, split, CAP, model_width).sum(axis=1)
+    chip_sum = swapped.astype(jnp.float32).sum(axis=0).astype(jnp.bfloat16)
+    returned = lax.all_to_all(chip_sum, ("req", "y"), split_axis=0, concat_axis=0, tiled=True)
+    summed = returned.astype(jnp.float32).reshape(EXPERTS, halves, CAP, model_width).sum(axis=1)
     summed = summed.reshape(EXPERTS * CAP, model_width)
     picked_rows = jnp.take(summed, flat_slot, axis=0).reshape(tok_rows, TOPK, model_width)
     moe_sum = jnp.sum(weights[:, :, None] * picked_rows, axis=1)
@@ -148,25 +151,28 @@
 
 
 def solution(mesh):
+    n_req, n_exp = mesh.devices.shape
+    fine = jax.sharding.Mesh(mesh.devices.reshape(n_req, n_exp // 2, 2), ("req", "y", "c"))
+    tok = ("req", "y", "c")
     return jax.shard_map(
         per_device,
-        mesh=mesh,
+        mesh=fine,
         in_specs=(
-            P(("req", "exp"), None),
+            P(tok, None),
             P(),
-            P(None, "exp"),
-            P(None, "exp"),
-            P(None, "exp"),
-            P("exp"),
-            P("exp", None),
+            P(None, ("y", "c")),
+            P(None, ("y", "c")),
+            P(None, ("y", "c")),
+            P(("y", "c")),
+            P(("y", "c"), None),
             P(),
             P(),
-            P(("req", "exp"), None),
+            P(tok, None),
             P("req", None),
-            P(("req", "exp"), None, None),
-            P(("req", "exp"), None, None),
-            P(("req", "exp"), None, None),
+            P(tok, None, None),
+            P(tok, None, None),
+            P(tok, None, None),
         ),
-        out_specs=P(("req", "exp"), None),
+        out_specs=P(tok, None),
         check_vma=False,
     )

time: 594 us -> 614 us (1.034)
  local copies, waits for them, and re-layouts: 85.3 us -> 131 us
  blocking collectives: 145 us -> 106 us
    all_to_all x1, waiting for transfers between devices: 143 us -> 76.9 us  [per_device(): lax.all_to_all(chip_sum, ('req', 'y'), split_axis=0, concat_axis=0, tiled...]
    all_to_all x1 -> x2, blocking collectives: 145 us -> 106 us  [the longest x1 92.3 us: per_device(): lax.all_to_all(send_rows, ('req', 'y'), split_axis=0, concat_axis=0, tile...]
    all_gather x1 -> x3, waiting for transfers between devices: 31.8 us -> 70.2 us  [the longest x1 33.6 us: per_device(): by_chip = lax.all_gather(normed_input, 'y', axis=0, tiled=False)]
    unnamed x2 -> x6, waiting for transfers between devices: 0.03 us -> 35.3 us
    reshape x2 -> x4, local copies, waits for them, and re-layouts: 29.8 us -> 44.3 us  [the longest x2 25.1 us: per_device(): slice_out.reshape(both.shape)]
    all_gather x0 -> x1, local copies, waits for them, and re-layouts: none -> 13.6 us  [per_device(): both = lax.all_gather(received, 'c', axis=0, tiled=False)]
    reduce_sum x0 -> x1, local copies, waits for them, and re-layouts: none -> 8 us  [per_device(): chip_sum = swapped.astype(jnp.float32).sum(axis=0).astype(jnp.bfloat16)]
    reduce_sum x1 -> x2, other arithmetic: 9.77 us -> 16.7 us  [the longest x1 9.65 us: per_device(): chip_sum = swapped.astype(jnp.float32).sum(axis=0).astype(jnp.bfloat16)]
  transfers between devices with their start and end apart: 3 -> 6, of which waited for: 3 -> 6; matrix products, arithmetic and copies ran while one was open for 2% -> 2% of each run, Pallas kernels for 0% -> 0%
where the time goes in v1:
time: 614 us; the launch traced here: 605 us
  waiting for transfers between devices  212 us (35%)
  local copies, waits for them, and re-layouts  131 us (21%)
  blocking collectives  106 us (17%)
  matrix products  83.4 us (14%)
  other arithmetic  46.8 us (8%)
  between operations  13.9 us (2%)
  starting transfers between devices  11.3 us (2%)
    all_to_all x1, blocking collectives, per_device(): lax.all_to_all(send_rows, ('req', 'y'), split_axis=0, concat_axis=0, tile...  92.3 us
    all_to_all x1, waiting for transfers between devices, per_device(): lax.all_to_all(chip_sum, ('req', 'y'), split_axis=0, concat_axis=0, tiled...  76.9 us
    unnamed x6, waiting for transfers between devices  35.3 us
    all_gather x1, waiting for transfers between devices, per_device(): by_chip = lax.all_gather(normed_input, 'y', axis=0, tiled=False)  33.6 us
    reduce_scatter x1, waiting for transfers between devices, per_device(): lax.psum_scatter(on_chip.reshape(n_y, tok_rows, model_width), 'y', scatte...  29.5 us
    dot_general x1, matrix products, per_device(): jnp.dot(hidden, expert_down[0], preferred_element_type=jnp.float32)  27.3 us
    reshape x2, local copies, waits for them, and re-layouts, per_device(): slice_out.reshape(both.shape)  25.1 us
    all_gather x1, waiting for transfers between devices, per_device(): both = lax.all_gather(received, 'c', axis=0, tiled=False)  23.4 us
  transfers between devices with their start and end apart: 6, of which 6 were waited for; matrix products, arithmetic and copies ran while one was open for 2% of the time, Pallas kernels for 0%

profile of v1, /device:TPU:10, one launch (start us, length us, event | category | flops | bytes accessed | tf_op | source)
XLA Modules:
  0.0 604.9 jit_solution(8165540641719783037)
XLA Ops:
  10.1 33.6 %all-gather.8.cloned.1.call-done = bf16[384,2880]{1,0:T(8,128)(2,1)} async-done(((bf16[96,2880]{1,0:T(8,128)(2,1)}), bf16[384,2880]{1,0:T(8,128)(2,1)}) %all-gather.8.cloned.1.call-update) | async-done | bytes 2211856 | tf_op jit(solution)/shard_map/all_gather | solution.py:57
  43.8 4.6 copy.109
  50.2 13.1 %all-gather.6.cloned.1.call-done = bf16[4,192,2880]{2,1,0:T(8,128)(2,1)} async-done(((bf16[4,96,2880]{2,1,0:T(8,128)(2,1)}), bf16[4,192,2880]{2,1,0:T(8,128)(2,1)}) %all-gather.6.cloned.1.call-update) | async-done | bytes 4423696 | tf_op jit(solution)/shard_map/all_gather | solution.py:58
  67.8 4.5 fusion.59
  72.5 8.1 %fusion = (f32[8,768]{1,0:T(8,128)S(1)}, f32[768,768,8]{1,0,2:T(8,128)}) fusion(pred[768,768]{0,1:T(8,128)(4,1)S(1)} %fusion.13, bf16[768,8,32]{0,2,1:T(8,128)(2,1)S(1)} %get-tuple-element.10, bf16[768,8,32]{0,2,1:T(8,128)(2,1)S(1)} %get-tuple-element.9, bf16[768,32]{0,1:T(8,128)(2,1)S(1)} %get-tuple-element.12, bf16[768,32]{0,1:T(8,128)(2,1)S(1)} %get-tuple-element.11), kind=kOutput, calls=%fused_computation.4 | convolution fusion | flops 619898880 | bytes 20373504 | tf_op jit(solution)/shard_map/qcgd,kcd->cgqk/dot_general | solution.py:91
  82.0 10.8 %fusion.3 = f32[8,768]{1,0:T(8,128)} fusion(f32[768,768,8]{1,0,2:T(8,128)} %get-tuple-element.16, f32[8,768]{1,0:T(8,128)} %broadcast_maximum_fusion, pred[768,768]{0,1:T(8,128)(4,1)S(1)} %fusion.13), kind=kLoop, calls=%fused_computation.8 | loop fusion | flops 18868224 | bytes 19513344 | tf_op jit(solution)/shard_map/reduce_sum | solution.py:99
  94.2 14.4 %fusion.16 = bf16[64,8,768]{2,0,1:T(8,128)(2,1)} fusion(f32[8,768]{1,0:T(8,128)} %exponential_add_fusion, f32[8,768]{1,0:T(8,128)} %broadcast_maximum_fusion, f32[768,768,8]{1,0,2:T(8,128)} %get-tuple-element.16, pred[768,768]{0,1:T(8,128)(4,1)S(1)} %fusion.13, bf16[768,2880]{1,0:T(8,128)(2,1)} %bitcast.132, bf16[2880,64]{0,1:T(8,128)(2,1)} %param.18), kind=kOutput, calls=%fused_computation.31 | convolution fusion | flops 911130624 | bytes 25092096 | tf_op jit(solution)/shard_map/cgqk,kcd->qcgd/dot_general | solution.py:101
  108.6 5.6 convolution_convert_fusion.1
  114.2 6.6 %copy.112 = bf16[768,2880]{1,0:T(8,128)(2,1)} copy(bf16[768,2880]{0,1:T(8,128)(2,1)} %convolution_convert_fusion.1) | data formatting | bytes 8847360 | tf_op jit(solution)/shard_map/convert_element_type | solution.py:103
  121.5 35.2 %all-reduce.3.cloned.1.call-done = bf16[2,4,96,2880]{3,2,0,1:T(8,128)(2,1)} async-done(((bf16[2,4,96,2880]{3,2,0,1:T(8,128)(2,1)}), bf16[2,4,96,2880]{3,2,0,1:T(8,128)(2,1)}) %all-reduce.3.cloned.1.call-update) | async-done | bytes 4423696
  162.3 29.5 %reduce-scatter.3.cloned.1.call-done = bf16[1,96,2880]{2,1,0:T(8,128)(2,1)} async-done(((bf16[4,96,2880]{2,1,0:T(8,128)(2,1)}), bf16[1,96,2880]{2,1,0:T(8,128)(2,1)}) %reduce-scatter.3.cloned.1.call-update) | async-done | bytes 552976 | tf_op jit(solution)/shard_map/reduce_scatter | solution.py:108
  197.5 4.7 convolution_convert_fusion.2
  202.2 4.4 broadcast_in_dim.41
  208.8 92.3 %all_to_all.15 = bf16[64,14,2880]{2,1,0:T(8,128)(2,1)S(1)} all-to-all(bf16[64,14,2880]{2,1,0:T(8,128)(2,1)S(1)} %bitcast.129), channel_id=1, replica_groups=mesh['req'=16,'y'=4,'c'=2] {'req','y'}, dimensions={0} | all-to-all | bytes 10321920 | tf_op jit(solution)/shard_map/all_to_all | solution.py:132
  304.7 23.4 %all-gather.10.cloned.1.call-done = bf16[128,14,2880]{2,0,1:T(8,128)(2,1)} async-done(((bf16[64,14,2880]{2,0,1:T(8,128)(2,1)}), bf16[128,14,2880]{2,0,1:T(8,128)(2,1)}) %all-gather.10.cloned.1.call-update) | async-done | bytes 10321936 | tf_op jit(solution)/shard_map/all_gather | solution.py:133
  328.1 13.6 %copy.122 = bf16[128,14,2880]{2,1,0:T(8,128)(2,1)} copy(bf16[128,14,2880]{2,0,1:T(8,128)(2,1)} %all-gather.10.cloned.1.call-done) | data formatting | bytes 20643840 | tf_op jit(solution)/shard_map/all_gather | solution.py:133
  341.7 15.4 %reshape.432 = bf16[1792,2880]{1,0:T(8,128)(2,1)} reshape(bf16[128,14,2880]{2,1,0:T(8,128)(2,1)} %copy.122) | data formatting | bytes 20643840 | tf_op jit(solution)/shard_map/reshape | solution.py:134
  357.1 14.6 %fusion.7 = f32[1792,720]{0,1:T(8,128)} fusion(bf16[1792,2880]{1,0:T(8,128)(2,1)} %reshape.432, bf16[1,2880,720]{1,2,0:T(8,128)(2,1)} %param.25), kind=kOutput, calls=%fused_computation.18 | convolution fusion | flops 7431782400 | bytes 19630080 | tf_op jit(solution)/shard_map/dot_general | solution.py:135
  371.7 27.3 %convolution_convert_fusion = bf16[1792,2880]{0,1:T(8,128)(2,1)} fusion(bf16[1,720,2880]{2,1,0:T(8,128)(2,1)} %param.27, f32[1792,720]{0,1:T(8,128)} %fusion.7, bf16[1792,2880]{1,0:T(8,128)(2,1)} %reshape.432, bf16[1,2880,720]{1,2,0:T(8,128)(2,1)} %param.26), kind=kOutput, calls=%fused_computation.10 | convolution fusion | flops 14879047680 | bytes 34099200 | tf_op jit(solution)/shard_map/dot_general | solution.py:138
  399.0 14.5 %copy.123 = bf16[1792,2880]{1,0:T(8,128)(2,1)} copy(bf16[1792,2880]{0,1:T(8,128)(2,1)} %convolution_convert_fusion) | data formatting | bytes 20643840 | tf_op jit(solution)/shard_map/convert_element_type | solution.py:138
  413.4 14.4 %reshape.433 = bf16[2,64,14,2880]{3,2,1,0:T(8,128)(2,1)} reshape(bf16[1792,2880]{1,0:T(8,128)(2,1)} %copy.123) | data formatting | bytes 20643840 | tf_op jit(solution)/shard_map/reshape | solution.py:142
  427.8 10.7 %copy.124 = bf16[2,64,14,2880]{3,1,2,0:T(8,128)(2,1)S(1)} copy(bf16[2,64,14,2880]{3,2,1,0:T(8,128)(2,1)} %reshape.433) | data formatting | bytes 20643840 | tf_op jit(solution)/shard_map/reshape | solution.py:142
  438.5 14.0 %all_to_all.16 = bf16[2,64,14,2880]{3,1,2,0:T(8,128)(2,1)} all-to-all(bf16[2,64,14,2880]{3,1,2,0:T(8,128)(2,1)S(1)} %copy.124), channel_id=1, replica_groups=mesh['req'=16,'y'=4,'c'=2] {'c'}, dimensions={0} | all-to-all | bytes 20643840 | tf_op jit(solution)/shard_map/all_to_all | solution.py:141
  452.5 9.7 %reduce_sum.105 = bf16[64,14,2880]{2,0,1:T(8,128)(2,1)} reduce(bf16[2,64,14,2880]{3,1,2,0:T(8,128)(2,1)} %all_to_all.16, bf16[]{:T(256)} %constant.70.clone.1), dimensions={0}, to_apply=%region_14.15 | reduce | flops 2580480 | bytes 15482882 | tf_op jit(solution)/shard_map/reduce_sum | solution.py:144
  462.1 8.0 %copy.125 = bf16[64,14,2880]{2,1,0:T(8,128)(2,1)} copy(bf16[64,14,2880]{2,0,1:T(8,128)(2,1)} %reduce_sum.105) | data formatting | bytes 10321920 | tf_op jit(solution)/shard_map/reduce_sum | solution.py:144
  470.1 11.1 %all-to-all-start.2 = ((bf16[64,14,2880]{2,1,0:T(8,128)(2,1)}), bf16[64,14,2880]{2,1,0:T(8,128)(2,1)}, u32[]{:S(2)}, u32[]{:S(2)}) async-start(bf16[64,14,2880]{2,1,0:T(8,128)(2,1)} %copy.125), calls=%async_computation.3 | async-start | bytes 12058624 | tf_op jit(solution)/shard_map/all_to_all | solution.py:145
  486.2 76.9 %all-to-all-done.2 = bf16[64,14,2880]{2,1,0:T(8,128)(2,1)} async-done(((bf16[64,14,2880]{2,1,0:T(8,128)(2,1)}), bf16[64,14,2880]{2,1,0:T(8,128)(2,1)}, u32[]{:S(2)}, u32[]{:S(2)}) %all-to-all-start.2) | async-done | bytes 5160992 | tf_op jit(solution)/shard_map/all_to_all | solution.py:145
  563.1 7.0 %convert_reduce_fusion = f32[32,14,2880]{2,1,0:T(8,128)} fusion(bf16[64,14,2880]{2,1,0:T(8,128)(2,1)} %all-to-all-done.2), kind=kLoop, calls=%fused_computation.9 | loop fusion | flops 3870720 | bytes 10321920 | tf_op jit(solution)/shard_map/reduce_sum | solution.py:146
  570.1 5.7 reshape.436
  575.8 9.0 %gather_fusion = f32[384,2880]{1,0:T(8,128)} fusion(f32[448,2880]{1,0:T(8,128)} %reshape.436, s32[1024]{0:T(1024)S(1)} %pad_clamp_fusion), kind=kCustom, calls=%fused_computation | custom fusion | bytes 8848896 | tf_op jit(solution)/shard_map/jit(_take)/gather | solution.py:148
  584.8 5.5 gather.12
  590.4 6.5 %multiply_reduce_fusion = f32[96,2880]{1,0:T(8,128)S(1)} fusion(f32[96,4,2880]{2,1,0:T(4,128)} %gather.12, f32[96,4]{1,0:T(8,128)} %copy.115, pred[96,4]{1,0:T(8,128)(4,1)S(1)} %copy.120), kind=kLoop, calls=%fused_computation.15 | loop fusion | flops 3041280 | bytes 5531520 | tf_op jit(solution)/shard_map/reduce_sum | solution.py:149
  (92 shorter events, 36.1 us)
Async XLA Ops:
  6.5 102.1 %copy-start = (bf16[512,2880]{0,1:T(8,128)(2,1)S(1)}, bf16[512,2880]{0,1:T(8,128)(2,1)}, u32[]{:S(2)}) copy-start(bf16[512,2880]{0,1:T(8,128)(2,1)} %param.20) | copy-start | bytes 8847364
  6.5 37.2 %all-gather.8.cloned.1.call-start = ((), (), s32[]{:S(2)}) async-start(), calls=%async_computation.6 | async-start | bytes 2826240 | tf_op jit(solution)/shard_map/all_gather | solution.py:57
  10.0 38.4 %copy-start.12 = (s32[1,6]{1,0:T(1,128)S(1)}, s32[1,6]{1,0:T(1,128)}, u32[]{:S(2)}) copy-start(s32[1,6]{1,0:T(1,128)} %param.24) | copy-start | bytes 76
  10.1 53.3 %all-gather.6.cloned.1.call-start = ((), (), s32[]{:S(2)}) async-start(), calls=%async_computation.4 | async-start | bytes 6782976 | tf_op jit(solution)/shard_map/all_gather | solution.py:58
  43.8 112.9 %all-reduce.3.cloned.1.call-start = ((), (), s32[]{:S(2)}) async-start(), calls=%async_computation.8 | async-start | bytes 9043968
  63.4 4.4 copy-start.4
  67.7 4.6 copy-start.5
  67.7 4.6 copy-start.6
  72.5 8.8 %copy-start.11 = (f32[8]{0:T(128)S(1)}, f32[8]{0:T(128)}, u32[]{:S(2)}) copy-start(f32[8]{0:T(128)} %param.19) | copy-start | bytes 100
  80.7 0.6 copy-start.7
  114.2 6.7 %copy-start.13 = (u32[128]{0:T(128)S(1)}, u32[128]{0:T(128)}, u32[]{:S(2)}) copy-start(u32[128]{0:T(128)} %constant.92) | copy-start | bytes 1540
  120.8 39.8 %copy-start.9 = (s32[96,4]{0,1:T(4,128)S(1)}, s32[96,4]{0,1:T(4,128)}, u32[]{:S(2)}) copy-start(s32[96,4]{0,1:T(4,128)} %param.23) | copy-start | bytes 4612
  120.8 71.0 %copy-start.2 = (bf16[96,2880]{1,0:T(8,128)(2,1)S(1)}, bf16[96,2880]{1,0:T(8,128)(2,1)}, u32[]{:S(2)}) copy-start(bf16[96,2880]{1,0:T(8,128)(2,1)} %param.14) | copy-start | bytes 1658884
  120.8 72.3 %copy-start.10 = (f32[2880]{0:T(1024)S(1)}, f32[2880]{0:T(1024)}, u32[]{:S(2)}) copy-start(f32[2880]{0:T(1024)} %param.21) | copy-start | bytes 34564
  120.9 70.9 %reduce-scatter.3.cloned.1.call-start = ((), (), s32[]{:S(2)}) async-start(), calls=%async_computation.5 | async-start | bytes 2826240 | tf_op jit(solution)/shard_map/reduce_scatter | solution.py:108
  160.6 167.5 %all-gather.10.cloned.1.call-start = ((), (), s32[]{:S(2)}) async-start(), calls=%async_computation.7 | async-start | bytes 15826944 | tf_op jit(solution)/shard_map/all_gather | solution.py:133
  470.1 11.9 %copy-start.8 = (bf16[2880,32]{0,1:T(8,128)(2,1)S(1)}, bf16[2880,32]{0,1:T(8,128)(2,1)}, u32[]{:S(2)}) copy-start(bf16[2880,32]{0,1:T(8,128)(2,1)} %param.22) | copy-start | bytes 552964
  470.1 93.0 %all-to-all-start.2 = ((bf16[64,14,2880]{2,1,0:T(8,128)(2,1)}), bf16[64,14,2880]{2,1,0:T(8,128)(2,1)}, u32[]{:S(2)}, u32[]{:S(2)}) async-start(bf16[64,14,2880]{2,1,0:T(8,128)(2,1)} %copy.125), calls=%async_computation.3 | async-start | bytes 12058624 | tf_op jit(solution)/shard_map/all_to_all | solution.py:145
  584.8 13.1 %copy-start.1 = (bf16[512,2880]{0,1:T(8,128)(2,1)S(1)}, bf16[512,2880]{0,1:T(8,128)(2,1)}, u32[]{:S(2)}) copy-start(bf16[512,2880]{0,1:T(8,128)(2,1)} %param.20) | copy-start | bytes 8847364
  590.4 6.5 %copy-start.3 = (bf16[1,96,2880]{2,1,0:T(8,128)(2,1)S(1)}, bf16[1,96,2880]{2,1,0:T(8,128)(2,1)}, u32[]{:S(2)}) copy-start(bf16[1,96,2880]{2,1,0:T(8,128)(2,1)} %reduce-scatter.3.cloned.1.call-done) | copy-start | bytes 1658884
Sparse Core Ops, SparseCore 0:
  10.2 33.5 all-gather.7
  45.4 17.8 all-gather.5
  120.9 35.7 all-reduce.2
  160.7 31.0 reduce-scatter.2
  304.8 23.2 all-gather.9

commit v2 on v1

--- a/solution.py
+++ b/solution.py
@@ -9,6 +9,7 @@
 EXPERTS = 32
 TOPK = 4
 CAP = 14
+ROWS = 16
 
 
 def rms_norm(value_rows, gain):
@@ -54,8 +55,7 @@
     local_kv = key_weight.shape[1] // HEAD_DIM
     head_group = QUERY_HEADS // KEY_VALUE_HEADS
     normed_input = rms_norm(tokens.astype(jnp.float32), attn_gain).astype(jnp.bfloat16)
-    by_chip = lax.all_gather(normed_input, "y", axis=0, tiled=False)
-    piece = lax.all_gather(by_chip, "c", axis=1, tiled=True).reshape(-1, model_width)
+    piece = lax.all_gather(normed_input, ("y", "c"), axis=0, tiled=True)
     projected = jnp.concatenate(
         [
             jnp.dot(piece, w_query, preferred_element_type=jnp.float32),
@@ -100,14 +100,12 @@
     probs = (expo / denom).astype(jnp.bfloat16)
     attended = jnp.einsum("cgqk,kcd->qcgd", probs, value_rows, preferred_element_type=jnp.float32)
     attended = attended.reshape(item_count, q_width).astype(jnp.bfloat16)
-    head_term = jnp.dot(attended, w_out, preferred_element_type=jnp.float32).astype(jnp.bfloat16)
-    n_y = lax.axis_size("y")
-    n_c = lax.axis_size("c")
-    head_term = head_term.reshape(n_y, n_c, tok_rows, model_width).transpose(1, 0, 2, 3)
-    on_chip = lax.psum_scatter(head_term, "c", scatter_dimension=0, tiled=True)
     attn_sum = lax.psum_scatter(
-        on_chip.reshape(n_y, tok_rows, model_width), "y", scatter_dimension=0, tiled=True
-    ).reshape(tok_rows, model_width).astype(jnp.float32)
+        jnp.dot(attended, w_out, preferred_element_type=jnp.float32).astype(jnp.bfloat16),
+        ("y", "c"),
+        scatter_dimension=0,
+        tiled=True,
+    ).astype(jnp.float32)
     residual = (tokens.astype(jnp.float32) + attn_sum).astype(jnp.bfloat16)
     normed2 = rms_norm(residual.astype(jnp.float32), ffn_gain).astype(jnp.bfloat16)
     logits = jnp.dot(normed2, router, preferred_element_type=jnp.float32)
@@ -118,35 +116,42 @@
     onehot_route = (flat_routes[:, None] == expert_ids[None, :]).astype(jnp.int32)
     rank = jnp.cumsum(onehot_route, axis=0) - 1
     slot_rank = jnp.sum(onehot_route * rank, axis=1)
-    flat_slot = flat_routes * CAP + slot_rank
-    slot_ids = jnp.arange(EXPERTS * CAP, dtype=jnp.int32)
-    dispatch_table = (slot_ids[:, None] == flat_slot[None, :]).astype(jnp.bfloat16)
-    repeated = jnp.repeat(normed2, TOPK, axis=0)
-    packed = jnp.dot(dispatch_table, repeated, preferred_element_type=jnp.float32).astype(
+    n_y = lax.axis_size("y")
+    halves = n_y // (EXPERTS // lax.axis_size("req"))
+    pos = (flat_routes[:, None] * halves + jnp.arange(halves, dtype=jnp.int32)[None, :]) * ROWS
+    pos = (pos + slot_rank[:, None]).reshape(tok_rows, TOPK, halves)
+    row_ids = jnp.arange(EXPERTS * halves * ROWS, dtype=jnp.int32)
+    match = pos[:, :, :, None] == row_ids[None, None, None, :]
+    dispatch_table = jnp.any(match, axis=(1, 2)).T.astype(jnp.bfloat16)
+    send_rows = jnp.dot(dispatch_table, normed2, preferred_element_type=jnp.float32).astype(
         jnp.bfloat16
+    ).reshape(EXPERTS * halves, ROWS, model_width)
+    combine = jnp.sum(jnp.where(match, weights[:, :, None, None], 0.0), axis=(1, 2))
+    received = lax.all_to_all(send_rows, ("req", "y"), split_axis=0, concat_axis=0, tiled=True)
+    swap = [(0, 1), (1, 0)]
+    sibling_rows = lax.ppermute(received, "c", perm=swap)
+
+    def expert_slice(rows):
+        flat = rows.reshape(-1, model_width)
+        gate = jnp.dot(flat, expert_gate[0], preferred_element_type=jnp.float32)
+        up_val = jnp.dot(flat, expert_up[0], preferred_element_type=jnp.float32)
+        hidden = ((up_val + 1.0) * gate * jax.nn.sigmoid(1.702 * gate)).astype(jnp.bfloat16)
+        return jnp.dot(hidden, expert_down[0], preferred_element_type=jnp.float32).astype(
+            jnp.bfloat16
+        )
+
+    own_out = expert_slice(received)
+    sibling_out = expert_slice(sibling_rows)
+    from_sibling = lax.ppermute(sibling_out, "c", perm=swap)
+    chip_sum = (own_out.astype(jnp.float32) + from_sibling.astype(jnp.float32)).astype(jnp.bfloat16)
+    returned = lax.all_to_all(
+        chip_sum.reshape(received.shape), ("req", "y"), split_axis=0, concat_axis=0, tiled=True
+    ).reshape(-1, model_width)
+    combine_hi = combine.astype(jnp.bfloat16)
+    combine_lo = (combine - combine_hi.astype(jnp.float32)).astype(jnp.bfloat16)
+    moe_sum = jnp.dot(combine_hi, returned, preferred_element_type=jnp.float32) + jnp.dot(
+        combine_lo, returned, preferred_element_type=jnp.float32
     )
-    halves = n_y // (EXPERTS // lax.axis_size("req"))
-    send_rows = jnp.broadcast_to(
-        packed.reshape(EXPERTS, 1, CAP, model_width), (EXPERTS, halves, CAP, model_width)
-    ).reshape(EXPERTS * halves, CAP, model_width)
-    received = lax.all_to_all(send_rows, ("req", "y"), split_axis=0, concat_axis=0, tiled=True)
-    both = lax.all_gather(received, "c", axis=0, tiled=False)
-    flat_rows = both.reshape(-1, model_width)
-    gate = jnp.dot(flat_rows, expert_gate[0], preferred_element_type=jnp.float32)
-    up_val = jnp.dot(flat_rows, expert_up[0], preferred_element_type=jnp.float32)
-    hidden = ((up_val + 1.0) * gate * jax.nn.sigmoid(1.702 * gate)).astype(jnp.bfloat16)
-    slice_out = jnp.dot(hidden, expert_down[0], preferred_element_type=jnp.float32).astype(
-        jnp.bfloat16
-    )
-    swapped = lax.all_to_all(
-        slice_out.reshape(both.shape), "c", split_axis=0, concat_axis=0, tiled=True
-    )
-    chip_sum = swapped.astype(jnp.float32).sum(axis=0).astype(jnp.bfloat16)
-    returned = lax.all_to_all(chip_sum, ("req", "y"), split_axis=0, concat_axis=0, tiled=True)
-    summed = returned.astype(jnp.float32).reshape(EXPERTS, halves, CAP, model_width).sum(axis=1)
-    summed = summed.reshape(EXPERTS * CAP, model_width)
-    picked_rows = jnp.take(summed, flat_slot, axis=0).reshape(tok_rows, TOPK, model_width)
-    moe_sum = jnp.sum(weights[:, :, None] * picked_rows, axis=1)
     return (residual.astype(jnp.float32) + moe_sum).astype(jnp.bfloat16)
 
 

time: 614 us -> 420 us (0.68)
  local copies, waits for them, and re-layouts: 131 us -> 27.5 us
  waiting for transfers between devices: 212 us -> 156 us
  blocking collectives: 106 us -> 82.2 us
  other arithmetic: 46.8 us -> 24.5 us
  matrix products: 83.4 us -> 98.1 us
    reshape x7 -> x0, local copies, waits for them, and re-layouts: 52.5 us -> none  [the longest x2 25.1 us: per_device(): slice_out.reshape(both.shape)]
    all_gather x3 -> x1, waiting for transfers between devices: 70.2 us -> 31.8 us  [per_device(): piece = lax.all_gather(normed_input, ('y', 'c'), axis=0, tiled=True)]
    unnamed x6 -> x2, waiting for transfers between devices: 35.3 us -> 0.03 us
    reduce_sum x3 -> x1, other arithmetic: 23.2 us -> 1.19 us  [per_device(): jnp.sum(jnp.where(match, weights[:, :, None, None], 0.0), axis=(1, 2))]
    gather x2 -> x0, local copies, waits for them, and re-layouts: 14.6 us -> none  [per_device(): jnp.take(summed, flat_slot, axis=0).reshape(tok_rows, TOPK, model_width)]
    dot_general x3 -> x8, matrix products: 46.5 us -> 61 us  [the longest x2 23.5 us: expert_slice(): jnp.dot(hidden, expert_down[0], preferred_element_type=jnp.float32)]
    all_to_all x1 -> x0, blocking collectives: 14 us -> none  [per_device(): lax.all_to_all(slice_out.reshape(both.shape), 'c', split_axis=0, concat_a...]
    all_gather x1 -> x0, local copies, waits for them, and re-layouts: 13.6 us -> none  [per_device(): both = lax.all_gather(received, 'c', axis=0, tiled=False)]
  transfers between devices with their start and end apart: 6 -> 5, of which waited for: 6 -> 4; matrix products, arithmetic and copies ran while one was open for 2% -> 6% of each run, Pallas kernels for 0% -> 0%
where the time goes in v2:
time: 420 us; the launch traced here: 412 us
  waiting for transfers between devices  156 us (37%)
  matrix products  98.1 us (23%)
  blocking collectives  82.2 us (20%)
  local copies, waits for them, and re-layouts  27.5 us (7%)
  other arithmetic  24.5 us (6%)
  between operations  14.2 us (3%)
  starting transfers between devices  9.05 us (2%)
    all_to_all x1, blocking collectives, per_device(): lax.all_to_all(send_rows, ('req', 'y'), split_axis=0, concat_axis=0, tile...  82.2 us
    all_to_all x1, waiting for transfers between devices, per_device(): lax.all_to_all(chip_sum.reshape(received.shape), ('req', 'y'), split_axis...  81.8 us
    reduce_scatter x1, waiting for transfers between devices, per_device(): lax.psum_scatter(jnp.dot(attended, w_out, preferred_element_type=jnp.floa...  32.9 us
    all_gather x1, waiting for transfers between devices, per_device(): piece = lax.all_gather(normed_input, ('y', 'c'), axis=0, tiled=True)  31.8 us
    dot_general x2, matrix products, expert_slice(): jnp.dot(hidden, expert_down[0], preferred_element_type=jnp.float32)  23.5 us
    dot_general x2, matrix products, expert_slice(): up_val = jnp.dot(flat, expert_up[0], preferred_element_type=jnp.float32)  17 us
    dot_general x1, matrix products, per_device(): jnp.einsum('cgqk,kcd->qcgd', probs, value_rows, preferred_element_type=jn...  14.1 us
    reduce_sum x1, other arithmetic, per_device(): jnp.sum(expo, axis=-1, keepdims=True) + jnp.exp(sink_score_logit - top)  10.8 us
  transfers between devices with their start and end apart: 5, of which 4 were waited for; matrix products, arithmetic and copies ran while one was open for 6% of the time, Pallas kernels for 0%

profile of v2, /device:TPU:10, one launch (start us, length us, event | category | flops | bytes accessed | tf_op | source)
XLA Modules:
  0.0 411.9 jit_solution(15117416671968286083)
XLA Ops:
  6.5 1.4 fusion.29
  8.0 2.1 fusion.31
  11.7 1.1 multiply_cosine_fusion
  13.2 31.8 %all-gather.2.cloned.1.call-done = bf16[768,2880]{1,0:T(8,128)(2,1)} async-done(((bf16[96,2880]{1,0:T(8,128)(2,1)}), bf16[768,2880]{1,0:T(8,128)(2,1)}) %all-gather.2.cloned.1.call-update) | async-done | bytes 4423696 | tf_op jit(solution)/shard_map/all_gather | solution.py:58
  45.0 3.9 convolution_bitcast_fusion
  49.4 4.6 %fusion.73 = f32[768,512]{0,1:T(8,128)S(1)} fusion(bf16[768,2880]{1,0:T(8,128)(2,1)S(1)} %copy-done.5, bf16[2880,512]{1,0:T(8,128)(2,1)} %param.16), kind=kOutput, calls=%fused_computation.113 | convolution fusion | flops 2264924160 | bytes 8945664 | tf_op jit(solution)/shard_map/dot_general | solution.py:61
  54.3 8.4 %fusion = (f32[8,768]{1,0:T(8,128)S(1)}, f32[768,768,8]{1,0,2:T(8,128)}) fusion(pred[768,768]{0,1:T(8,128)(4,1)S(1)} %fusion.19, bf16[768,8,32]{0,2,1:T(8,128)(2,1)S(1)} %get-tuple-element.12, bf16[768,8,32]{0,2,1:T(8,128)(2,1)S(1)} %get-tuple-element.11, bf16[768,32]{0,1:T(8,128)(2,1)S(1)} %get-tuple-element.14, bf16[768,32]{0,1:T(8,128)(2,1)S(1)} %get-tuple-element.13), kind=kOutput, calls=%fused_computation.3 | convolution fusion | flops 619898880 | bytes 20373504 | tf_op jit(solution)/shard_map/qcgd,kcd->cgqk/dot_general | solution.py:91
  63.9 10.8 %fusion.3 = f32[8,768]{1,0:T(8,128)} fusion(f32[768,768,8]{1,0,2:T(8,128)} %get-tuple-element.18, f32[8,768]{1,0:T(8,128)} %broadcast_maximum_fusion, pred[768,768]{0,1:T(8,128)(4,1)S(1)} %fusion.19), kind=kLoop, calls=%fused_computation.7 | loop fusion | flops 18868224 | bytes 19513344 | tf_op jit(solution)/shard_map/reduce_sum | solution.py:99
  74.7 1.4 exponential_add_fusion
  76.2 14.1 %fusion.26 = bf16[64,8,768]{2,0,1:T(8,128)(2,1)} fusion(f32[8,768]{1,0:T(8,128)} %exponential_add_fusion, f32[8,768]{1,0:T(8,128)} %broadcast_maximum_fusion, f32[768,768,8]{1,0,2:T(8,128)} %get-tuple-element.18, pred[768,768]{0,1:T(8,128)(4,1)S(1)} %fusion.19, bf16[768,2880]{1,0:T(8,128)(2,1)} %all-gather.2.cloned.1.call-done, bf16[2880,64]{0,1:T(8,128)(2,1)} %param.18), kind=kOutput, calls=%fused_computation.39 | convolution fusion | flops 911130624 | bytes 25092096 | tf_op jit(solution)/shard_map/cgqk,kcd->qcgd/dot_general | solution.py:101
  90.2 5.8 %convolution_convert_fusion.2 = bf16[768,2880]{1,0:T(8,128)(2,1)} fusion(bf16[768,512]{0,1:T(8,128)(2,1)} %bitcast.129, bf16[512,2880]{0,1:T(8,128)(2,1)S(1)} %copy-done), kind=kOutput, calls=%fused_computation.13 | convolution fusion | flops 2267136000 | bytes 8159232 | tf_op jit(solution)/shard_map/dot_general | solution.py:104
  97.1 1.1 reduce-window.11
  99.2 32.9 %reduce-scatter.2.cloned.1.call-done = bf16[96,2880]{1,0:T(8,128)(2,1)} async-done(((bf16[768,2880]{1,0:T(8,128)(2,1)}), bf16[96,2880]{1,0:T(8,128)(2,1)}) %reduce-scatter.2.cloned.1.call-update) | async-done | bytes 552976 | tf_op jit(solution)/shard_map/reduce_scatter | solution.py:103
  132.1 1.4 fusion.33
  133.5 4.4 %convolution_convert_fusion = bf16[1024,2880]{0,1:T(8,128)(2,1)} fusion(pred[96,1024]{1,0:T(8,128)(4,1)S(1)} %fusion.18, bf16[96,2880]{1,0:T(8,128)(2,1)S(1)} %get-tuple-element.10, f32[2880]{0:T(1024)S(1)} %copy-done.11, f32[96]{0:T(128)S(1)} %add_rsqrt_fusion), kind=kOutput, calls=%fused_computation.11 | convolution fusion | flops 570286080 | bytes 6561408 | tf_op jit(solution)/shard_map/dot_general | solution.py:126
  137.9 8.5 %copy.50 = bf16[1024,2880]{1,0:T(8,128)(2,1)} copy(bf16[1024,2880]{0,1:T(8,128)(2,1)} %convolution_convert_fusion) | data formatting | bytes 11796480 | tf_op jit(solution)/shard_map/convert_element_type | solution.py:126
  146.4 82.2 %all_to_all.10 = bf16[64,16,2880]{2,1,0:T(8,128)(2,1)S(1)} all-to-all(bf16[64,16,2880]{2,1,0:T(8,128)(2,1)} %bitcast.118), channel_id=1, replica_groups=mesh['req'=16,'y'=4,'c'=2] {'req','y'}, dimensions={0} | all-to-all | bytes 11796480 | tf_op jit(solution)/shard_map/all_to_all | solution.py:130
  228.6 2.6 copy-done.2
  231.2 9.8 %collective-permute-done = bf16[64,16,2880]{2,1,0:T(8,128)(2,1)S(1)} collective-permute-done((bf16[64,16,2880]{2,1,0:T(8,128)(2,1)S(1)}, bf16[64,16,2880]{2,1,0:T(8,128)(2,1)S(1)}, u32[]{:S(2)}, u32[]{:S(2)}) %collective-permute-start) | collective-permute-done | bytes 5898272 | tf_op jit(solution)/shard_map/ppermute | solution.py:132
  241.0 2.6 copy-done.13
  243.6 8.5 %fusion.12 = f32[1024,720]{0,1:T(8,128)} fusion(bf16[1024,2880]{1,0:T(8,128)(2,1)S(1)} %bitcast.124, bf16[1,2880,720]{1,2,0:T(8,128)(2,1)} %param.26), kind=kOutput, calls=%fused_computation.20 | convolution fusion | flops 4246732800 | bytes 12994560 | tf_op jit(solution)/shard_map/dot_general | solution.py:137
  252.1 16.5 %convolution_convert_fusion.1 = bf16[1024,2880]{0,1:T(8,128)(2,1)} fusion(bf16[1,720,2880]{2,1,0:T(8,128)(2,1)} %param.27, f32[1024,720]{0,1:T(8,128)} %fusion.12, bf16[1024,2880]{1,0:T(8,128)(2,1)} %bitcast.125, bf16[1,2880,720]{1,2,0:T(8,128)(2,1)} %param.25), kind=kOutput, calls=%fused_computation.12 | convolution fusion | flops 8502312960 | bytes 23040000 | tf_op jit(solution)/shard_map/dot_general | solution.py:139
  268.7 8.5 %fusion.14 = f32[1024,720]{0,1:T(8,128)S(1)} fusion(bf16[1024,2880]{1,0:T(8,128)(2,1)} %bitcast.119, bf16[1,2880,720]{1,2,0:T(8,128)(2,1)} %param.26), kind=kOutput, calls=%fused_computation.22 | convolution fusion | flops 4246732800 | bytes 12994560 | tf_op jit(solution)/shard_map/dot_general | solution.py:137
  277.2 7.4 %multiply_convert_fusion.1 = bf16[1024,720]{0,1:T(8,128)(2,1)S(1)} fusion(f32[1024,720]{0,1:T(8,128)S(1)} %fusion.14, bf16[1024,2880]{1,0:T(8,128)(2,1)S(1)} %bitcast.120, bf16[1,2880,720]{1,2,0:T(8,128)(2,1)} %param.25), kind=kOutput, calls=%fused_computation.31 | convolution fusion | flops 4252631040 | bytes 14469120 | tf_op jit(solution)/shard_map/dot_general | solution.py:136
  284.6 7.0 %add_convert_fusion = bf16[1024,2880]{0,1:T(8,128)(2,1)} fusion(bf16[1024,2880]{0,1:T(8,128)(2,1)S(1)} %collective-permute-done.1, bf16[1024,720]{0,1:T(8,128)(2,1)S(1)} %multiply_convert_fusion.1, bf16[1,720,2880]{2,1,0:T(8,128)(2,1)S(1)} %bitcast.127), kind=kOutput, calls=%fused_computation.8 | convolution fusion | flops 4261478400 | bytes 17418240 | tf_op jit(solution)/shard_map/dot_general | solution.py:139
  291.6 8.5 %copy.51 = bf16[1024,2880]{1,0:T(8,128)(2,1)} copy(bf16[1024,2880]{0,1:T(8,128)(2,1)} %add_convert_fusion) | data formatting | bytes 11796480 | tf_op jit(solution)/shard_map/convert_element_type | solution.py:146
  300.1 8.9 %all-to-all-start.1 = ((bf16[64,16,2880]{2,1,0:T(8,128)(2,1)}), bf16[64,16,2880]{2,1,0:T(8,128)(2,1)}, u32[]{:S(2)}, u32[]{:S(2)}) async-start(bf16[64,16,2880]{2,1,0:T(8,128)(2,1)} %bitcast.117), calls=%async_computation.2 | async-start | bytes 12058624 | tf_op jit(solution)/shard_map/all_to_all | solution.py:147
  309.6 2.9 gather_fusion
  312.8 1.2 select_reduce_fusion
  314.0 81.8 %all-to-all-done.1 = bf16[64,16,2880]{2,1,0:T(8,128)(2,1)} async-done(((bf16[64,16,2880]{2,1,0:T(8,128)(2,1)}), bf16[64,16,2880]{2,1,0:T(8,128)(2,1)}, u32[]{:S(2)}, u32[]{:S(2)}) %all-to-all-start.1) | async-done | bytes 5898272 | tf_op jit(solution)/shard_map/all_to_all | solution.py:147
  395.8 4.1 fusion.55
  399.9 4.7 %fusion.17 = bf16[96,2880]{1,0:T(8,128)(2,1)} fusion(f32[96,2880]{1,0:T(8,128)S(1)} %fusion.55, bf16[1024,2880]{1,0:T(8,128)(2,1)} %bitcast.26, bf16[96,2880]{1,0:T(8,128)(2,1)S(1)} %get-tuple-element.10, f32[96,1024]{1,0:T(8,128)S(1)} %copy-done.6), kind=kOutput, calls=%fused_computation.26 | convolution fusion | flops 567730176 | bytes 8503296 | tf_op jit(solution)/shard_map/dot_general | solution.py:152
  (72 shorter events, 7.0 us)
Async XLA Ops:
  6.5 83.7 %copy-start = (bf16[512,2880]{0,1:T(8,128)(2,1)S(1)}, bf16[512,2880]{0,1:T(8,128)(2,1)}, u32[]{:S(2)}) copy-start(bf16[512,2880]{0,1:T(8,128)(2,1)} %param.20) | copy-start | bytes 8847364
  6.5 38.5 %all-gather.2.cloned.1.call-start = ((), (), s32[]{:S(2)}) async-start(), calls=%async_computation.3 | async-start | bytes 5087232 | tf_op jit(solution)/shard_map/all_gather | solution.py:58
  10.1 122.1 %reduce-scatter.2.cloned.1.call-start = ((), (), s32[]{:S(2)}) async-start(), calls=%async_computation.4 | async-start | bytes 5087232 | tf_op jit(solution)/shard_map/reduce_scatter | solution.py:103
  45.0 4.4 %copy-start.5 = (bf16[768,2880]{1,0:T(8,128)(2,1)S(1)}, bf16[768,2880]{1,0:T(8,128)(2,1)}, u32[]{:S(2)}) copy-start(bf16[768,2880]{1,0:T(8,128)(2,1)} %all-gather.2.cloned.1.call-done) | copy-start | bytes 13271044
  49.4 4.7 %copy-start.7 = (f32[768,32]{0,1:T(8,128)S(1)}, f32[768,32]{0,1:T(8,128)}, u32[]{:S(2)}) copy-start(f32[768,32]{0,1:T(8,128)} %get-tuple-element.15) | copy-start | bytes 294916
  49.4 4.7 %copy-start.8 = (f32[768,32]{0,1:T(8,128)S(1)}, f32[768,32]{0,1:T(8,128)}, u32[]{:S(2)}) copy-start(f32[768,32]{0,1:T(8,128)} %get-tuple-element.16) | copy-start | bytes 294916
  54.3 9.0 %copy-start.12 = (f32[8]{0:T(128)S(1)}, f32[8]{0:T(128)}, u32[]{:S(2)}) copy-start(f32[8]{0:T(128)} %param.19) | copy-start | bytes 100
  62.6 0.6 copy-start.9
  96.1 0.7 copy-start.10
  96.1 36.1 %copy-start.4 = (bf16[96,2880]{1,0:T(8,128)(2,1)S(1)}, bf16[96,2880]{1,0:T(8,128)(2,1)}, u32[]{:S(2)}) copy-start(bf16[96,2880]{1,0:T(8,128)(2,1)} %param.14) | copy-start | bytes 1658884
  96.1 37.4 %copy-start.11 = (f32[2880]{0:T(1024)S(1)}, f32[2880]{0:T(1024)}, u32[]{:S(2)}) copy-start(f32[2880]{0:T(1024)} %param.21) | copy-start | bytes 34564
  228.6 2.6 copy-start.2
  231.2 9.8 %collective-permute-start = (bf16[64,16,2880]{2,1,0:T(8,128)(2,1)S(1)}, bf16[64,16,2880]{2,1,0:T(8,128)(2,1)S(1)}, u32[]{:S(2)}, u32[]{:S(2)}) collective-permute-start(bf16[64,16,2880]{2,1,0:T(8,128)(2,1)S(1)} %all_to_all.10), channel_id=1, source_target_pairs={{0,1},{1,0},{2,3},{3,2},{4,5},{5,4},{6,7},{7,6},{8,9},{9,8},{10,11... | collective-permute-start | bytes 17694728 | tf_op jit(solution)/shard_map/ppermute | solution.py:132
  241.0 2.6 copy-start.13
  268.6 16.0 %collective-permute-start.1 = (bf16[1024,2880]{0,1:T(8,128)(2,1)}, bf16[1024,2880]{0,1:T(8,128)(2,1)S(1)}, u32[]{:S(2)}, u32[]{:S(2)}) collective-permute-start(bf16[1024,2880]{0,1:T(8,128)(2,1)} %convolution_convert_fusion.1), channel_id=1, source_target_pairs={{0,1},{1,0},{2,3},{3,2},{4,5},{5,4},{6,7},{7,6},{8,9},{9,8},{10,11... | collective-permute-start | bytes 17694728 | tf_op jit(solution)/shard_map/ppermute | solution.py:145
  268.7 8.5 %copy-start.3 = (bf16[64,16,2880]{2,1,0:T(8,128)(2,1)S(1)}, bf16[64,16,2880]{2,1,0:T(8,128)(2,1)}, u32[]{:S(2)}) copy-start(bf16[64,16,2880]{2,1,0:T(8,128)(2,1)} %copy-done.2) | copy-start | bytes 17694724
  268.7 15.9 %slice-start = ((s8[4239360]{0:T(1024)(128)(4,1)}), s8[4194304]{0:T(1024)(128)(4,1)S(1)}, s32[]{:S(2)}) async-start(s8[4239360]{0:T(1024)(128)(4,1)} %bitcast.126), calls=%async_computation.5 | async-start | bytes 8388608
  277.2 7.4 %slice-start.1 = ((s8[4239360]{0:T(1024)(128)(4,1)}), s8[45056]{0:T(1024)(128)(4,1)S(1)}, s32[]{:S(2)}) async-start(s8[4239360]{0:T(1024)(128)(4,1)} %bitcast.126), calls=%async_computation.6 | async-start | bytes 90112
  300.1 9.1 %copy-start.14 = (bf16[2880,32]{0,1:T(8,128)(2,1)S(1)}, bf16[2880,32]{0,1:T(8,128)(2,1)}, u32[]{:S(2)}) copy-start(bf16[2880,32]{0,1:T(8,128)(2,1)} %param.22) | copy-start | bytes 552964
  300.1 95.6 %all-to-all-start.1 = ((bf16[64,16,2880]{2,1,0:T(8,128)(2,1)}), bf16[64,16,2880]{2,1,0:T(8,128)(2,1)}, u32[]{:S(2)}, u32[]{:S(2)}) async-start(bf16[64,16,2880]{2,1,0:T(8,128)(2,1)} %bitcast.117), calls=%async_computation.2 | async-start | bytes 12058624 | tf_op jit(solution)/shard_map/all_to_all | solution.py:147
  395.8 4.1 copy-start.6
  395.8 8.8 %copy-start.1 = (bf16[512,2880]{0,1:T(8,128)(2,1)S(1)}, bf16[512,2880]{0,1:T(8,128)(2,1)}, u32[]{:S(2)}) copy-start(bf16[512,2880]{0,1:T(8,128)(2,1)} %param.20) | copy-start | bytes 8847364
Sparse Core Ops, SparseCore 0:
  10.2 34.7 all-gather.1
  96.2 35.8 reduce-scatter.1

commit v3 on v2

--- a/solution.py
+++ b/solution.py
@@ -10,6 +10,7 @@
 TOPK = 4
 CAP = 14
 ROWS = 16
+CHUNK_ROWS = 8
 
 
 def rms_norm(value_rows, gain):
@@ -118,18 +119,13 @@
     slot_rank = jnp.sum(onehot_route * rank, axis=1)
     n_y = lax.axis_size("y")
     halves = n_y // (EXPERTS // lax.axis_size("req"))
-    pos = (flat_routes[:, None] * halves + jnp.arange(halves, dtype=jnp.int32)[None, :]) * ROWS
-    pos = (pos + slot_rank[:, None]).reshape(tok_rows, TOPK, halves)
-    row_ids = jnp.arange(EXPERTS * halves * ROWS, dtype=jnp.int32)
-    match = pos[:, :, :, None] == row_ids[None, None, None, :]
-    dispatch_table = jnp.any(match, axis=(1, 2)).T.astype(jnp.bfloat16)
-    send_rows = jnp.dot(dispatch_table, normed2, preferred_element_type=jnp.float32).astype(
-        jnp.bfloat16
-    ).reshape(EXPERTS * halves, ROWS, model_width)
-    combine = jnp.sum(jnp.where(match, weights[:, :, None, None], 0.0), axis=(1, 2))
-    received = lax.all_to_all(send_rows, ("req", "y"), split_axis=0, concat_axis=0, tiled=True)
+    chunks = ROWS // CHUNK_ROWS
+    pos = (flat_routes[:, None] * halves + jnp.arange(halves, dtype=jnp.int32)[None, :]) * CHUNK_ROWS
+    pos = (pos + (slot_rank % CHUNK_ROWS)[:, None]).reshape(tok_rows, TOPK, halves)
+    part_of = (slot_rank // CHUNK_ROWS).reshape(tok_rows, TOPK)
+    row_ids = jnp.arange(EXPERTS * halves * CHUNK_ROWS, dtype=jnp.int32)
+    placed = pos[:, :, :, None] == row_ids[None, None, None, :]
     swap = [(0, 1), (1, 0)]
-    sibling_rows = lax.ppermute(received, "c", perm=swap)
 
     def expert_slice(rows):
         flat = rows.reshape(-1, model_width)
@@ -140,18 +136,45 @@
             jnp.bfloat16
         )
 
-    own_out = expert_slice(received)
-    sibling_out = expert_slice(sibling_rows)
-    from_sibling = lax.ppermute(sibling_out, "c", perm=swap)
-    chip_sum = (own_out.astype(jnp.float32) + from_sibling.astype(jnp.float32)).astype(jnp.bfloat16)
-    returned = lax.all_to_all(
-        chip_sum.reshape(received.shape), ("req", "y"), split_axis=0, concat_axis=0, tiled=True
-    ).reshape(-1, model_width)
-    combine_hi = combine.astype(jnp.bfloat16)
-    combine_lo = (combine - combine_hi.astype(jnp.float32)).astype(jnp.bfloat16)
-    moe_sum = jnp.dot(combine_hi, returned, preferred_element_type=jnp.float32) + jnp.dot(
-        combine_lo, returned, preferred_element_type=jnp.float32
-    )
+    tables, combines, received = [], [], []
+    for part in range(chunks):
+        match = placed & (part_of == part)[:, :, None, None]
+        dispatch_table = jnp.any(match, axis=(1, 2)).T.astype(jnp.bfloat16)
+        send_rows = jnp.dot(dispatch_table, normed2, preferred_element_type=jnp.float32).astype(
+            jnp.bfloat16
+        ).reshape(EXPERTS * halves, CHUNK_ROWS, model_width)
+        combines.append(jnp.sum(jnp.where(match, weights[:, :, None, None], 0.0), axis=(1, 2)))
+        received.append(
+            lax.all_to_all(send_rows, ("req", "y"), split_axis=0, concat_axis=0, tiled=True)
+        )
+    chip_sums, returned = [], []
+    for part in range(chunks):
+        rows = received[part]
+        if part > 0:
+            rows, chip_sums[-1] = lax.optimization_barrier((rows, chip_sums[-1]))
+            returned.append(
+                lax.all_to_all(chip_sums[-1], ("req", "y"), split_axis=0, concat_axis=0, tiled=True)
+            )
+        sibling_rows = lax.ppermute(rows, "c", perm=swap)
+        own_out = expert_slice(rows)
+        sibling_out = expert_slice(sibling_rows)
+        from_sibling = lax.ppermute(sibling_out, "c", perm=swap)
+        chip_sum = (own_out.astype(jnp.float32) + from_sibling.astype(jnp.float32)).astype(
+            jnp.bfloat16
+        )
+        chip_sums.append(chip_sum.reshape(rows.shape))
+        if part > 0:
+            returned[-1], chip_sums[-1] = lax.optimization_barrier((returned[-1], chip_sums[-1]))
+    returned.append(
+        lax.all_to_all(chip_sums[-1], ("req", "y"), split_axis=0, concat_axis=0, tiled=True)
+    )
+    moe_sum = jnp.zeros((tok_rows, model_width), jnp.float32)
+    for combine, back in zip(combines, returned):
+        back = back.reshape(-1, model_width)
+        combine_hi = combine.astype(jnp.bfloat16)
+        combine_lo = (combine - combine_hi.astype(jnp.float32)).astype(jnp.bfloat16)
+        moe_sum = moe_sum + jnp.dot(combine_hi, back, preferred_element_type=jnp.float32)
+        moe_sum = moe_sum + jnp.dot(combine_lo, back, preferred_element_type=jnp.float32)
     return (residual.astype(jnp.float32) + moe_sum).astype(jnp.bfloat16)
 
 

time: 420 us -> 405 us (0.964)
  blocking collectives: 82.2 us -> 50.2 us
  matrix products: 98.1 us -> 119 us
  waiting for transfers between devices: 156 us -> 136 us
  starting transfers between devices: 9.05 us -> 28.4 us
  local copies, waits for them, and re-layouts: 27.5 us -> 23.1 us
    all_to_all x1, blocking collectives: 82.2 us -> 50.2 us  [per_device(): lax.all_to_all(send_rows, ('req', 'y'), split_axis=0, concat_axis=0, tile...]
    all_to_all x1 -> x3, waiting for transfers between devices: 81.8 us -> 60.4 us  [the longest x2 43 us: per_device(): lax.all_to_all(chip_sums[-1], ('req', 'y'), split_axis=0, concat_axis=0,...]
    all_to_all x1 -> x3, starting transfers between devices: 8.85 us -> 28 us  [the longest x2 20.3 us: per_device(): lax.all_to_all(chip_sums[-1], ('req', 'y'), split_axis=0, concat_axis=0,...]
    dot_general x2 -> x4, matrix products: 23.5 us -> 41.9 us  [expert_slice(): jnp.dot(hidden, expert_down[0], preferred_element_type=jnp.float32)]
    dot_general x2, matrix products: 17 us -> 10.5 us  [expert_slice(): up_val = jnp.dot(flat, expert_up[0], preferred_element_type=jnp.float32)]
    dot_general x1 -> x2, matrix products: 7.35 us -> 13.5 us  [expert_slice(): gate = jnp.dot(flat, expert_gate[0], preferred_element_type=jnp.float32)]
    dot_general x2 -> x4, matrix products: 8.78 us -> 12.3 us  [the longest x2 6.87 us: per_device(): jnp.dot(combine_lo, back, preferred_element_type=jnp.float32)]
    convert_element_type x1 -> x2, local copies, waits for them, and re-layouts: 8.5 us -> 6.04 us  [per_device(): (own_out.astype(jnp.float32) + from_sibling.astype(jnp.float32)).astype(j...]
  transfers between devices with their start and end apart: 5 -> 9, of which waited for: 4 -> 7; matrix products, arithmetic and copies ran while one was open for 6% -> 16% of each run, Pallas kernels for 0% -> 0%
where the time goes in v3:
time: 405 us; the launch traced here: 398 us
  waiting for transfers between devices  136 us (34%)
  matrix products  119 us (29%)
  blocking collectives  50.2 us (12%)
  starting transfers between devices  28.4 us (7%)
  other arithmetic  26.4 us (7%)
  local copies, waits for them, and re-layouts  23.1 us (6%)
  between operations  14.2 us (4%)
    all_to_all x1, blocking collectives, per_device(): lax.all_to_all(send_rows, ('req', 'y'), split_axis=0, concat_axis=0, tile...  50.2 us
    all_to_all x2, waiting for transfers between devices, per_device(): lax.all_to_all(chip_sums[-1], ('req', 'y'), split_axis=0, concat_axis=0,...  43 us
    dot_general x4, matrix products, expert_slice(): jnp.dot(hidden, expert_down[0], preferred_element_type=jnp.float32)  41.9 us
    reduce_scatter x1, waiting for transfers between devices, per_device(): lax.psum_scatter(jnp.dot(attended, w_out, preferred_element_type=jnp.floa...  32.3 us
    all_gather x1, waiting for transfers between devices, per_device(): piece = lax.all_gather(normed_input, ('y', 'c'), axis=0, tiled=True)  31.8 us
    all_to_all x2, starting transfers between devices, per_device(): lax.all_to_all(chip_sums[-1], ('req', 'y'), split_axis=0, concat_axis=0,...  20.3 us
    all_to_all x1, waiting for transfers between devices, per_device(): lax.all_to_all(send_rows, ('req', 'y'), split_axis=0, concat_axis=0, tile...  17.4 us
    dot_general x1, matrix products, per_device(): jnp.einsum('cgqk,kcd->qcgd', probs, value_rows, preferred_element_type=jn...  14.1 us
  transfers between devices with their start and end apart: 9, of which 7 were waited for; matrix products, arithmetic and copies ran while one was open for 16% of the time, Pallas kernels for 0%

profile of v3, /device:TPU:10, one launch (start us, length us, event | category | flops | bytes accessed | tf_op | source)
XLA Modules:
  0.0 397.5 jit_solution(14931621161806972218)
XLA Ops:
  13.2 31.8 %all-gather.2.cloned.1.call-done = bf16[768,2880]{1,0:T(8,128)(2,1)} async-done(((bf16[96,2880]{1,0:T(8,128)(2,1)}), bf16[768,2880]{1,0:T(8,128)(2,1)}) %all-gather.2.cloned.1.call-update) | async-done | bytes 4423696 | tf_op jit(solution)/shard_map/all_gather | solution.py:59
  45.0 3.9 convolution_bitcast_fusion
  49.4 4.6 %fusion.141 = f32[768,512]{0,1:T(8,128)S(1)} fusion(bf16[768,2880]{1,0:T(8,128)(2,1)S(1)} %copy-done.6, bf16[2880,512]{1,0:T(8,128)(2,1)} %param.16), kind=kOutput, calls=%fused_computation.174 | convolution fusion | flops 2264924160 | bytes 8945664 | tf_op jit(solution)/shard_map/dot_general | solution.py:62
  54.3 8.7 %fusion = (f32[8,768]{1,0:T(8,128)S(1)}, f32[768,768,8]{1,0,2:T(8,128)}) fusion(pred[768,768]{0,1:T(8,128)(4,1)S(1)} %fusion.45, bf16[768,8,32]{0,2,1:T(8,128)(2,1)S(1)} %get-tuple-element.24, bf16[768,8,32]{0,2,1:T(8,128)(2,1)S(1)} %get-tuple-element.23, bf16[768,32]{0,1:T(8,128)(2,1)S(1)} %get-tuple-element.26, bf16[768,32]{0,1:T(8,128)(2,1)S(1)} %get-tuple-element.25), kind=kOutput, calls=%fused_computation.3 | convolution fusion | flops 619898880 | bytes 20373504 | tf_op jit(solution)/shard_map/qcgd,kcd->cgqk/dot_general | solution.py:92
  64.2 10.8 %fusion.3 = f32[8,768]{1,0:T(8,128)} fusion(f32[768,768,8]{1,0,2:T(8,128)} %get-tuple-element.30, f32[8,768]{1,0:T(8,128)} %broadcast_maximum_fusion, pred[768,768]{0,1:T(8,128)(4,1)S(1)} %fusion.45), kind=kLoop, calls=%fused_computation.7 | loop fusion | flops 18868224 | bytes 19513344 | tf_op jit(solution)/shard_map/reduce_sum | solution.py:100
  76.5 14.1 %fusion.50 = bf16[64,8,768]{2,0,1:T(8,128)(2,1)} fusion(f32[8,768]{1,0:T(8,128)} %exponential_add_fusion, f32[8,768]{1,0:T(8,128)} %broadcast_maximum_fusion, f32[768,768,8]{1,0,2:T(8,128)} %get-tuple-element.30, pred[768,768]{0,1:T(8,128)(4,1)S(1)} %fusion.45, bf16[768,2880]{1,0:T(8,128)(2,1)} %all-gather.2.cloned.1.call-done, bf16[2880,64]{0,1:T(8,128)(2,1)} %param.18), kind=kOutput, calls=%fused_computation.75 | convolution fusion | flops 911130624 | bytes 25092096 | tf_op jit(solution)/shard_map/cgqk,kcd->qcgd/dot_general | solution.py:102
  90.5 5.8 %convolution_convert_fusion = bf16[768,2880]{1,0:T(8,128)(2,1)} fusion(bf16[768,512]{0,1:T(8,128)(2,1)} %bitcast.193, bf16[512,2880]{0,1:T(8,128)(2,1)S(1)} %copy-done), kind=kOutput, calls=%fused_computation.12 | convolution fusion | flops 2267136000 | bytes 8159232 | tf_op jit(solution)/shard_map/dot_general | solution.py:105
  100.1 32.3 %reduce-scatter.2.cloned.1.call-done = bf16[96,2880]{1,0:T(8,128)(2,1)} async-done(((bf16[768,2880]{1,0:T(8,128)(2,1)}), bf16[96,2880]{1,0:T(8,128)(2,1)}) %reduce-scatter.2.cloned.1.call-update) | async-done | bytes 552976 | tf_op jit(solution)/shard_map/reduce_scatter | solution.py:104
  137.6 3.0 copy.63
  140.6 50.2 %all_to_all.20 = bf16[64,8,2880]{2,1,0:T(8,128)(2,1)S(1)} all-to-all(bf16[64,8,2880]{2,1,0:T(8,128)(2,1)} %bitcast.188), channel_id=1, replica_groups=mesh['req'=16,'y'=4,'c'=2] {'req','y'}, dimensions={0} | all-to-all | bytes 5898240 | tf_op jit(solution)/shard_map/all_to_all | solution.py:148
  192.5 5.5 %collective-permute-done = bf16[64,8,2880]{2,1,0:T(8,128)(2,1)S(1)} collective-permute-done((bf16[64,8,2880]{2,1,0:T(8,128)(2,1)S(1)}, bf16[64,8,2880]{2,1,0:T(8,128)(2,1)S(1)}, u32[]{:S(2)}, u32[]{:S(2)}) %collective-permute-start) | collective-permute-done | bytes 2949152 | tf_op jit(solution)/shard_map/ppermute | solution.py:158
  199.6 4.7 %fusion.22 = f32[512,720]{0,1:T(8,128)S(1)} fusion(bf16[1,2880,720]{1,2,0:T(8,128)(2,1)} %param.26, bf16[64,8,2880]{2,1,0:T(8,128)(2,1)S(1)} %collective-permute-done), kind=kOutput, calls=%fused_computation.35 | convolution fusion | flops 2123366400 | bytes 8570880 | tf_op jit(solution)/shard_map/dot_general | solution.py:133
  204.3 11.0 %convolution_convert_fusion.3 = bf16[512,2880]{0,1:T(8,128)(2,1)} fusion(bf16[1,720,2880]{2,1,0:T(8,128)(2,1)} %param.27, f32[512,720]{0,1:T(8,128)S(1)} %fusion.22, bf16[1,2880,720]{1,2,0:T(8,128)(2,1)} %param.25, bf16[64,8,2880]{2,1,0:T(8,128)(2,1)} %copy-done.16), kind=kOutput, calls=%fused_computation.15 | convolution fusion | flops 4251156480 | bytes 15667200 | tf_op jit(solution)/shard_map/dot_general | solution.py:135
  217.5 3.1 copy.62
  220.5 7.7 %all-to-all-start = ((bf16[64,8,2880]{2,1,0:T(8,128)(2,1)}), bf16[64,8,2880]{2,1,0:T(8,128)(2,1)}, u32[]{:S(2)}, u32[]{:S(2)}) async-start(bf16[64,8,2880]{2,1,0:T(8,128)(2,1)} %bitcast.187), calls=%async_computation.1 | async-start | bytes 6029312 | tf_op jit(solution)/shard_map/all_to_all | solution.py:148
  228.2 6.7 %fusion.16 = f32[512,720]{0,1:T(8,128)} fusion(bf16[1,2880,720]{1,2,0:T(8,128)(2,1)} %param.25, bf16[64,8,2880]{2,1,0:T(8,128)(2,1)} %copy-done.7), kind=kOutput, calls=%fused_computation.29 | convolution fusion | flops 2123366400 | bytes 8570880 | tf_op jit(solution)/shard_map/dot_general | solution.py:132
  235.0 10.6 %add_convert_fusion.1 = bf16[512,2880]{0,1:T(8,128)(2,1)S(1)} fusion(bf16[512,2880]{0,1:T(8,128)(2,1)} %collective-permute-done.1, bf16[1,720,2880]{2,1,0:T(8,128)(2,1)} %param.27, f32[512,720]{0,1:T(8,128)} %fusion.16, bf16[1,2880,720]{1,2,0:T(8,128)(2,1)} %param.26, bf16[64,8,2880]{2,1,0:T(8,128)(2,1)} %copy-done.7), kind=kOutput, calls=%fused_computation.11 | convolution fusion | flops 4257054720 | bytes 18616320 | tf_op jit(solution)/shard_map/dot_general | solution.py:135
  245.6 3.0 copy.64
  248.6 17.4 %all-to-all-done = bf16[64,8,2880]{2,1,0:T(8,128)(2,1)} async-done(((bf16[64,8,2880]{2,1,0:T(8,128)(2,1)}), bf16[64,8,2880]{2,1,0:T(8,128)(2,1)}, u32[]{:S(2)}, u32[]{:S(2)}) %all-to-all-start) | async-done | bytes 2949152 | tf_op jit(solution)/shard_map/all_to_all | solution.py:148
  266.0 5.7 %collective-permute-done.2 = bf16[64,8,2880]{2,1,0:T(8,128)(2,1)S(1)} collective-permute-done((bf16[64,8,2880]{2,1,0:T(8,128)(2,1)}, bf16[64,8,2880]{2,1,0:T(8,128)(2,1)S(1)}, u32[]{:S(2)}, u32[]{:S(2)}) %collective-permute-start.2) | collective-permute-done | bytes 2949152 | tf_op jit(solution)/shard_map/ppermute | solution.py:158
  273.4 5.8 %fusion.18 = f32[512,720]{0,1:T(8,128)} fusion(bf16[1,2880,720]{1,2,0:T(8,128)(2,1)} %param.26, bf16[64,8,2880]{2,1,0:T(8,128)(2,1)S(1)} %collective-permute-done.2), kind=kOutput, calls=%fused_computation.31 | convolution fusion | flops 2123366400 | bytes 8570880 | tf_op jit(solution)/shard_map/dot_general | solution.py:133
  279.2 9.8 %convolution_convert_fusion.1 = bf16[512,2880]{0,1:T(8,128)(2,1)S(1)} fusion(bf16[1,720,2880]{2,1,0:T(8,128)(2,1)} %param.27, f32[512,720]{0,1:T(8,128)} %fusion.18, bf16[1,2880,720]{1,2,0:T(8,128)(2,1)} %param.25, bf16[64,8,2880]{2,1,0:T(8,128)(2,1)} %copy-done.17), kind=kOutput, calls=%fused_computation.13 | convolution fusion | flops 4251156480 | bytes 15667200 | tf_op jit(solution)/shard_map/dot_general | solution.py:135
  289.2 10.7 %all-to-all-start.2 = ((bf16[64,8,2880]{2,1,0:T(8,128)(2,1)}), bf16[64,8,2880]{2,1,0:T(8,128)(2,1)}, u32[]{:S(2)}, u32[]{:S(2)}) async-start(bf16[64,8,2880]{2,1,0:T(8,128)(2,1)} %bitcast.186), calls=%async_computation.3 | async-start | bytes 6029312 | tf_op jit(solution)/shard_map/all_to_all | solution.py:156
  299.9 6.8 %fusion.12 = f32[512,720]{0,1:T(8,128)} fusion(bf16[1,2880,720]{1,2,0:T(8,128)(2,1)} %param.25, bf16[64,8,2880]{2,1,0:T(8,128)(2,1)} %all-to-all-done), kind=kOutput, calls=%fused_computation.25 | convolution fusion | flops 2123366400 | bytes 8570880 | tf_op jit(solution)/shard_map/dot_general | solution.py:132
  306.7 10.6 %add_convert_fusion = bf16[512,2880]{0,1:T(8,128)(2,1)S(1)} fusion(bf16[512,2880]{0,1:T(8,128)(2,1)} %collective-permute-done.3, bf16[1,720,2880]{2,1,0:T(8,128)(2,1)} %param.27, f32[512,720]{0,1:T(8,128)} %fusion.12, bf16[1,2880,720]{1,2,0:T(8,128)(2,1)} %param.26, bf16[64,8,2880]{2,1,0:T(8,128)(2,1)} %all-to-all-done), kind=kOutput, calls=%fused_computation.10 | convolution fusion | flops 4257054720 | bytes 18616320 | tf_op jit(solution)/shard_map/dot_general | solution.py:135
  317.3 3.0 copy.65
  320.3 17.2 %all-to-all-done.2 = bf16[64,8,2880]{2,1,0:T(8,128)(2,1)} async-done(((bf16[64,8,2880]{2,1,0:T(8,128)(2,1)}), bf16[64,8,2880]{2,1,0:T(8,128)(2,1)}, u32[]{:S(2)}, u32[]{:S(2)}) %all-to-all-start.2) | async-done | bytes 2949152 | tf_op jit(solution)/shard_map/all_to_all | solution.py:156
  337.5 9.6 %all-to-all-start.3 = ((bf16[64,8,2880]{2,1,0:T(8,128)(2,1)}), bf16[64,8,2880]{2,1,0:T(8,128)(2,1)}, u32[]{:S(2)}, u32[]{:S(2)}) async-start(bf16[64,8,2880]{2,1,0:T(8,128)(2,1)} %bitcast.185), calls=%async_computation.4 | async-start | bytes 6029312 | tf_op jit(solution)/shard_map/all_to_all | solution.py:169
  354.6 3.5 convolution_add_fusion.2
  358.0 25.8 %all-to-all-done.3 = bf16[64,8,2880]{2,1,0:T(8,128)(2,1)} async-done(((bf16[64,8,2880]{2,1,0:T(8,128)(2,1)}), bf16[64,8,2880]{2,1,0:T(8,128)(2,1)}, u32[]{:S(2)}, u32[]{:S(2)}) %all-to-all-start.3) | async-done | bytes 2949152 | tf_op jit(solution)/shard_map/all_to_all | solution.py:169
  383.8 3.0 convolution_add_fusion.1
  386.9 3.4 fusion.31
  (92 shorter events, 33.7 us)
Async XLA Ops:
  6.5 84.0 %copy-start = (bf16[512,2880]{0,1:T(8,128)(2,1)S(1)}, bf16[512,2880]{0,1:T(8,128)(2,1)}, u32[]{:S(2)}) copy-start(bf16[512,2880]{0,1:T(8,128)(2,1)} %param.20) | copy-start | bytes 8847364
  6.5 38.5 %all-gather.2.cloned.1.call-start = ((), (), s32[]{:S(2)}) async-start(), calls=%async_computation.5 | async-start | bytes 5087232 | tf_op jit(solution)/shard_map/all_gather | solution.py:59
  10.1 122.3 %reduce-scatter.2.cloned.1.call-start = ((), (), s32[]{:S(2)}) async-start(), calls=%async_computation.6 | async-start | bytes 5087232 | tf_op jit(solution)/shard_map/reduce_scatter | solution.py:104
  45.0 4.4 %copy-start.6 = (bf16[768,2880]{1,0:T(8,128)(2,1)S(1)}, bf16[768,2880]{1,0:T(8,128)(2,1)}, u32[]{:S(2)}) copy-start(bf16[768,2880]{1,0:T(8,128)(2,1)} %all-gather.2.cloned.1.call-done) | copy-start | bytes 13271044
  49.4 4.7 %copy-start.9 = (f32[768,32]{0,1:T(8,128)S(1)}, f32[768,32]{0,1:T(8,128)}, u32[]{:S(2)}) copy-start(f32[768,32]{0,1:T(8,128)} %get-tuple-element.27) | copy-start | bytes 294916
  49.4 4.7 %copy-start.10 = (f32[768,32]{0,1:T(8,128)S(1)}, f32[768,32]{0,1:T(8,128)}, u32[]{:S(2)}) copy-start(f32[768,32]{0,1:T(8,128)} %get-tuple-element.28) | copy-start | bytes 294916
  54.3 9.3 %copy-start.15 = (f32[8]{0:T(128)S(1)}, f32[8]{0:T(128)}, u32[]{:S(2)}) copy-start(f32[8]{0:T(128)} %param.19) | copy-start | bytes 100
  62.9 0.6 copy-start.11
  96.4 0.7 copy-start.13
  96.4 36.1 %copy-start.2 = (bf16[96,2880]{1,0:T(8,128)(2,1)S(1)}, bf16[96,2880]{1,0:T(8,128)(2,1)}, u32[]{:S(2)}) copy-start(bf16[96,2880]{1,0:T(8,128)(2,1)} %param.14) | copy-start | bytes 1658884
  96.4 37.4 %copy-start.14 = (f32[2880]{0:T(1024)S(1)}, f32[2880]{0:T(1024)}, u32[]{:S(2)}) copy-start(f32[2880]{0:T(1024)} %param.21) | copy-start | bytes 34564
  135.1 0.8 copy-start.3
  190.9 1.7 copy-start.7
  192.5 5.5 %collective-permute-start = (bf16[64,8,2880]{2,1,0:T(8,128)(2,1)S(1)}, bf16[64,8,2880]{2,1,0:T(8,128)(2,1)S(1)}, u32[]{:S(2)}, u32[]{:S(2)}) collective-permute-start(bf16[64,8,2880]{2,1,0:T(8,128)(2,1)S(1)} %all_to_all.20), channel_id=1, source_target_pairs={{0,1},{1,0},{2,3},{3,2},{4,5},{5,4},{6,7},{7,6},{8,9},{9,8},{10,11... | collective-permute-start | bytes 8847368 | tf_op jit(solution)/shard_map/ppermute | solution.py:158
  198.0 1.6 copy-start.16
  215.3 19.7 %collective-permute-start.1 = (bf16[512,2880]{0,1:T(8,128)(2,1)}, bf16[512,2880]{0,1:T(8,128)(2,1)}, u32[]{:S(2)}, u32[]{:S(2)}) collective-permute-start(bf16[512,2880]{0,1:T(8,128)(2,1)} %convolution_convert_fusion.3), channel_id=1, source_target_pairs={{0,1},{1,0},{2,3},{3,2},{4,5},{5,4},{6,7},{7,6},{8,9},{9,8},{10,11... | collective-permute-start | bytes 8847368 | tf_op jit(solution)/shard_map/ppermute | solution.py:161
  220.5 45.5 %all-to-all-start = ((bf16[64,8,2880]{2,1,0:T(8,128)(2,1)}), bf16[64,8,2880]{2,1,0:T(8,128)(2,1)}, u32[]{:S(2)}, u32[]{:S(2)}) async-start(bf16[64,8,2880]{2,1,0:T(8,128)(2,1)} %bitcast.187), calls=%async_computation.1 | async-start | bytes 6029312 | tf_op jit(solution)/shard_map/all_to_all | solution.py:148
  266.0 5.7 %collective-permute-start.2 = (bf16[64,8,2880]{2,1,0:T(8,128)(2,1)}, bf16[64,8,2880]{2,1,0:T(8,128)(2,1)S(1)}, u32[]{:S(2)}, u32[]{:S(2)}) collective-permute-start(bf16[64,8,2880]{2,1,0:T(8,128)(2,1)} %all-to-all-done), channel_id=1, source_target_pairs={{0,1},{1,0},{2,3},{3,2},{4,5},{5,4},{6,7},{7,6},{8,9},{9,8},{10,11... | collective-permute-start | bytes 8847368 | tf_op jit(solution)/shard_map/ppermute | solution.py:158
  271.7 1.7 copy-start.17
  289.0 17.7 %collective-permute-start.3 = (bf16[512,2880]{0,1:T(8,128)(2,1)S(1)}, bf16[512,2880]{0,1:T(8,128)(2,1)}, u32[]{:S(2)}, u32[]{:S(2)}) collective-permute-start(bf16[512,2880]{0,1:T(8,128)(2,1)S(1)} %convolution_convert_fusion.1), channel_id=1, source_target_pairs={{0,1},{1,0},{2,3},{3,2},{4,5},{5,4},{6,7},{7,6},{8,9},{9,8},{10,11... | collective-permute-start | bytes 8847368 | tf_op jit(solution)/shard_map/ppermute | solution.py:161
  289.2 48.3 %all-to-all-start.2 = ((bf16[64,8,2880]{2,1,0:T(8,128)(2,1)}), bf16[64,8,2880]{2,1,0:T(8,128)(2,1)}, u32[]{:S(2)}, u32[]{:S(2)}) async-start(bf16[64,8,2880]{2,1,0:T(8,128)(2,1)} %bitcast.186), calls=%async_computation.3 | async-start | bytes 6029312 | tf_op jit(solution)/shard_map/all_to_all | solution.py:156
  337.5 9.8 %copy-start.4 = (bf16[96,2880]{1,0:T(8,128)(2,1)S(1)}, bf16[96,2880]{1,0:T(8,128)(2,1)}, u32[]{:S(2)}) copy-start(bf16[96,2880]{1,0:T(8,128)(2,1)} %copy-done.3) | copy-start | bytes 1658884
  337.5 9.8 %copy-start.12 = (bf16[2880,32]{0,1:T(8,128)(2,1)S(1)}, bf16[2880,32]{0,1:T(8,128)(2,1)}, u32[]{:S(2)}) copy-start(bf16[2880,32]{0,1:T(8,128)(2,1)} %param.22) | copy-start | bytes 552964
  337.5 46.3 %all-to-all-start.3 = ((bf16[64,8,2880]{2,1,0:T(8,128)(2,1)}), bf16[64,8,2880]{2,1,0:T(8,128)(2,1)}, u32[]{:S(2)}, u32[]{:S(2)}) async-start(bf16[64,8,2880]{2,1,0:T(8,128)(2,1)} %bitcast.185), calls=%async_computation.4 | async-start | bytes 6029312 | tf_op jit(solution)/shard_map/all_to_all | solution.py:169
  383.8 3.0 copy-start.5
  383.8 3.0 copy-start.8
  383.8 6.4 %copy-start.1 = (bf16[512,2880]{0,1:T(8,128)(2,1)S(1)}, bf16[512,2880]{0,1:T(8,128)(2,1)}, u32[]{:S(2)}) copy-start(bf16[512,2880]{0,1:T(8,128)(2,1)} %param.20) | copy-start | bytes 8847364
Sparse Core Ops, SparseCore 0:
  10.2 34.7 all-gather.1
  96.5 35.8 reduce-scatter.1
